TPU v7x, 32 devices: a whole 2x2x4 slice. The times are simulated.
32 devices in a mesh: tile: 8 (over z, x), rows: 4 (over y, core).
Axes of the slice: x: 2, y: 2, z: 4, core: 2. Of those that a mesh axis runs over, the one named last changes fastest.
Arguments:
- adjoint_rows: bfloat16 [2048, 128, 128], P('rows', 'tile'), may hold values from -6 to 6
- panel_index: int32 [2, 64], P(None, 'rows'), may hold values from 0 to 511
- coef_class: int32 [8], P('tile'), may hold values from 0 to 7
- class_gain: float32 [8], replicated, may hold values from 0.25 to 1
- cell_coef: float32 [128, 128], P('tile'), may hold values from 0.3 to 1
Outputs:
- hessian: float32 [2, 64, 2048], P(None, 'tile', 'rows')
Inputs may be any that keep to these rules, and one draw needn't show every extreme that they name: `panel_index`: panel row j is taken from row block j // 16; the entry is its offset in that block.
All inputs are finite; a program needn't handle non-finite values.
Results may differ from a plain program's by a relative error of at most 0.00081.
Values may be sent and summed in bfloat16 or wider, within the bound.
No kernel may reach another device: no remote copies, remote signals or barrier semaphores. Data moves between devices by JAX's collectives and lax.ppermute only.
A program may use at most 64 MiB of HBM per device.

v0:
```python
import math

import jax
import jax.numpy as jnp
from jax import lax
from jax.sharding import PartitionSpec as P

SMOOTH = 4


def padded_2(cells, sides, width):
    for axis, dim in sides:
        count = lax.axis_size(axis)
        ends = count - 1
        head = lax.slice_in_dim(cells, 0, width, axis=dim)
        tail = lax.slice_in_dim(cells, cells.shape[dim] - width, cells.shape[dim], axis=dim)
        cells = jnp.concatenate(
            [
                lax.ppermute(tail, axis, [(i, (i + 1) % count) for i in range(ends)]),
                cells,
                lax.ppermute(head, axis, [((i + 1) % count, i) for i in range(ends)]),
            ],
            axis=dim,
        )
    return cells


def step_core(padded, coef_pad):
    middle = padded[..., 1:-1, :]
    coef_mid = coef_pad[1:-1, :]
    face_up = 0.5 * (coef_pad[:-2, :] + coef_mid)
    face_down = 0.5 * (coef_pad[2:, :] + coef_mid)
    side_vals = jnp.pad(middle, [(0, 0)] * (middle.ndim - 1) + [(1, 1)])
    side_coef = jnp.pad(coef_mid, ((0, 0), (1, 1)))
    face_left = 0.5 * (side_coef[:, :-2] + coef_mid)
    face_right = 0.5 * (side_coef[:, 2:] + coef_mid)
    result = middle + face_up * (padded[..., :-2, :] - middle)
    result = result + face_down * (padded[..., 2:, :] - middle)
    result = result + face_left * (side_vals[..., :-2] - middle)
    return result + face_right * (side_vals[..., 2:] - middle)


def per_device(adjoint_rows, panel_index, coef_class, class_gain, cell_coef):
    resident = adjoint_rows.shape[0]
    lines = cell_coef.shape[0]
    cells = cell_coef.shape[1]
    panel_count = panel_index.shape[0]
    per_block = panel_index.shape[1]
    classes = jnp.arange(class_gain.shape[0], dtype=jnp.int32)
    own_gain = jnp.sum(jnp.where(classes == coef_class[0], class_gain, 0.0))
    diffusivity = 0.2 * own_gain * cell_coef
    picked = jnp.take(adjoint_rows, panel_index.reshape(-1), axis=0)
    state = picked.astype(jnp.float32).reshape(panel_count, per_block, lines, cells)
    coef_pad = padded_2(diffusivity, (("tile", 0),), 1)
    for sweep_no in range(SMOOTH):
        padded = padded_2(state, (("tile", 2),), 1)
        state = step_core(padded, coef_pad)
    smoothed = state.astype(jnp.bfloat16)
    flat_rows = adjoint_rows.reshape(resident, lines * cells)
    gram_scale = 1.0 / math.sqrt(lax.axis_size("tile") * lines * cells)
    rows_piece = lax.all_gather(smoothed, "rows", axis=1, tiled=True)
    flat_piece = rows_piece.reshape(-1, lines * cells)
    product = lax.dot_general(
        flat_piece, flat_rows, (((1,), (1,)), ((), ())), preferred_element_type=jnp.float32
    )
    terms = (product * gram_scale).reshape(rows_piece.shape[0], rows_piece.shape[1], resident)
    return lax.psum_scatter(terms, "tile", scatter_dimension=1, tiled=True)


def solution(mesh):
    return jax.shard_map(
        per_device,
        mesh=mesh,
        in_specs=(P("rows", "tile", None), P(None, "rows"), P("tile"), P(), P("tile", None)),
        out_specs=P(None, "tile", "rows"),
        check_vma=False,
    )
```

profile of v0, /device:TPU:0, one launch (start us, length us, event | category | flops | bytes accessed | tf_op | source)
XLA Modules:
  0.0 136.7 jit_solution(222297486784417046)
XLA Ops:
  7.3 1.3 fusion.61
  9.3 0.7 broadcast_multiply_fusion
  10.0 4.8 %collective-permute-start = (f32[1,128]{1,0:T(1,128)S(1)}, f32[1,128]{1,0:T(1,128)S(1)}, u32[]{:S(2)}, u32[]{:S(2)}) collective-permute-start(f32[1,128]{1,0:T(1,128)S(1)} %get-tuple-element.17), channel_id=1, source_target_pairs={{0,4},{4,8},{8,12},{12,16},{16,20},{20,24},{24,28},{1,5},{5,9},{9,... | collective-permute-start | bytes 1544 | tf_op jit(solution)/shard_map/ppermute | solution.py:19
  14.8 1.3 collective-permute-start.2
  16.1 0.7 compare_and_fusion
  16.8 0.8 reshape.53
  17.6 2.2 %gather_fusion = bf16[32,16,128]{2,1,0:T(8,128)(2,1)S(1)} fusion(bf16[512,16,128]{2,1,0:T(8,128)(2,1)} %param.5, s32[1024]{0:T(1024)S(1)} %pad_clamp_fusion), kind=kCustom, calls=%fused_computation | custom fusion | bytes 262272 | tf_op jit(solution)/shard_map/jit(_take)/gather | solution.py:52
  19.8 0.1 fusion.52
  19.9 4.5 %collective-permute-start.1 = (f32[2,16,1,128]{3,2,1,0:T(1,128)S(1)}, f32[2,16,1,128]{3,2,1,0:T(1,128)S(1)}, u32[]{:S(2)}, u32[]{:S(2)}) collective-permute-start(f32[2,16,1,128]{3,2,1,0:T(1,128)S(1)} %get-tuple-element.11), channel_id=1, source_target_pairs={{0,4},{4,8},{8,12},{12,16},{16,20},{20,24},{24,28},{1,5},{5,9},{9,... | collective-permute-start | bytes 49160 | tf_op jit(solution)/shard_map/ppermute | solution.py:19
  24.5 1.3 collective-permute-start.3
  25.8 0.1 fusion.60
  25.9 0.0 collective-permute-done.1
  25.9 4.6 %collective-permute-done.3 = f32[2,16,1,128]{3,2,1,0:T(1,128)S(1)} collective-permute-done((f32[2,16,1,128]{3,2,1,0:T(1,128)S(1)}, f32[2,16,1,128]{3,2,1,0:T(1,128)S(1)}, u32[]{:S(2)}, u32[]{:S(2)}) %collective-permute-start.3) | collective-permute-done | bytes 16416 | tf_op jit(solution)/shard_map/ppermute | solution.py:21
  30.5 0.3 fusion.11
  30.9 4.8 %collective-permute-start.4 = (f32[2,16,1,128]{3,2,1,0:T(1,128)S(1)}, f32[2,16,1,128]{3,2,1,0:T(1,128)S(1)}, u32[]{:S(2)}, u32[]{:S(2)}) collective-permute-start(f32[2,16,1,128]{3,2,1,0:T(1,128)S(1)} %get-tuple-element.9), channel_id=1, source_target_pairs={{0,4},{4,8},{8,12},{12,16},{16,20},{20,24},{24,28},{1,5},{5,9},{9,... | collective-permute-start | bytes 49160 | tf_op jit(solution)/shard_map/ppermute | solution.py:19
  35.7 1.3 collective-permute-start.5
  37.0 0.1 collective-permute-done.4
  37.1 4.2 %collective-permute-done.5 = f32[2,16,1,128]{3,2,1,0:T(1,128)S(1)} collective-permute-done((f32[2,16,1,128]{3,2,1,0:T(1,128)S(1)}, f32[2,16,1,128]{3,2,1,0:T(1,128)S(1)}, u32[]{:S(2)}, u32[]{:S(2)}) %collective-permute-start.5) | collective-permute-done | bytes 16416 | tf_op jit(solution)/shard_map/ppermute | solution.py:21
  41.3 0.2 fusion.18
  41.6 2.9 %collective-permute-start.6 = (f32[2,16,1,128]{3,2,1,0:T(1,128)S(1)}, f32[2,16,1,128]{3,2,1,0:T(1,128)S(1)}, u32[]{:S(2)}, u32[]{:S(2)}) collective-permute-start(f32[2,16,1,128]{3,2,1,0:T(1,128)S(1)} %get-tuple-element.7), channel_id=1, source_target_pairs={{0,4},{4,8},{8,12},{12,16},{16,20},{20,24},{24,28},{1,5},{5,9},{9,... | collective-permute-start | bytes 49160 | tf_op jit(solution)/shard_map/ppermute | solution.py:19
  44.5 1.3 collective-permute-start.7
  45.8 0.1 collective-permute-done.6
  45.9 4.2 %collective-permute-done.7 = f32[2,16,1,128]{3,2,1,0:T(1,128)S(1)} collective-permute-done((f32[2,16,1,128]{3,2,1,0:T(1,128)S(1)}, f32[2,16,1,128]{3,2,1,0:T(1,128)S(1)}, u32[]{:S(2)}, u32[]{:S(2)}) %collective-permute-start.7) | collective-permute-done | bytes 16416 | tf_op jit(solution)/shard_map/ppermute | solution.py:21
  50.2 0.2 fusion.24
  50.4 4.9 %collective-permute-start.8 = (f32[2,16,1,128]{3,2,1,0:T(1,128)S(1)}, f32[2,16,1,128]{3,2,1,0:T(1,128)S(1)}, u32[]{:S(2)}, u32[]{:S(2)}) collective-permute-start(f32[2,16,1,128]{3,2,1,0:T(1,128)S(1)} %get-tuple-element.5), channel_id=1, source_target_pairs={{0,4},{4,8},{8,12},{12,16},{16,20},{20,24},{24,28},{1,5},{5,9},{9,... | collective-permute-start | bytes 49160 | tf_op jit(solution)/shard_map/ppermute | solution.py:19
  55.3 1.3 collective-permute-start.9
  56.6 0.1 collective-permute-done.8
  56.8 4.2 %collective-permute-done.9 = f32[2,16,1,128]{3,2,1,0:T(1,128)S(1)} collective-permute-done((f32[2,16,1,128]{3,2,1,0:T(1,128)S(1)}, f32[2,16,1,128]{3,2,1,0:T(1,128)S(1)}, u32[]{:S(2)}, u32[]{:S(2)}) %collective-permute-start.9) | collective-permute-done | bytes 16416 | tf_op jit(solution)/shard_map/ppermute | solution.py:21
  61.0 0.2 fusion.31
  61.2 7.2 %all_gather.3 = bf16[2,64,16,128]{3,2,1,0:T(8,128)(2,1)S(1)} all-gather(bf16[2,16,16,128]{3,2,1,0:T(8,128)(2,1)S(1)} %fusion.31), channel_id=1, replica_groups=mesh['tile'=8,'rows'=4] {'rows'}, dimensions={1}, use_global_device_ids=true | all-gather | bytes 655360 | tf_op jit(solution)/shard_map/all_gather | solution.py:61
  68.4 1.5 %fusion.3 = f32[128,512]{1,0:T(8,128)} fusion(bf16[64,8,16,128]{3,2,1,0:T(8,128)(2,1)S(1)} %bitcast.21, bf16[16,8,16,128]{3,2,1,0:T(8,128)(2,1)S(1)} %bitcast.19), kind=kOutput, calls=%fused_computation.4 | convolution fusion | flops 268500992 | bytes 2883584 | tf_op jit(solution)/shard_map/dot_general | solution.py:63
  69.9 59.9 %reduce-scatter.2.cloned.1.call-done = f32[2,8,512]{2,1,0:T(8,128)} async-done(((f32[2,64,512]{2,1,0:T(8,128)}), f32[2,8,512]{2,1,0:T(8,128)}) %reduce-scatter.2.cloned.1.call-update) | async-done | bytes 32784 | tf_op jit(solution)/shard_map/reduce_scatter | solution.py:67
  (13 shorter events, 0.1 us)
Async XLA Ops:
  6.5 61.8 %copy-start = (bf16[512,16,128]{2,1,0:T(8,128)(2,1)S(1)}, bf16[512,16,128]{2,1,0:T(8,128)(2,1)}, u32[]{:S(2)}) copy-start(bf16[512,16,128]{2,1,0:T(8,128)(2,1)} %param.5) | copy-start | bytes 6291460
  6.5 123.3 %reduce-scatter.2.cloned.1.call-start = ((), (), s32[]{:S(2)}) async-start(), calls=%async_computation.1 | async-start | bytes 294912 | tf_op jit(solution)/shard_map/reduce_scatter | solution.py:67
  10.0 15.8 %collective-permute-start = (f32[1,128]{1,0:T(1,128)S(1)}, f32[1,128]{1,0:T(1,128)S(1)}, u32[]{:S(2)}, u32[]{:S(2)}) collective-permute-start(f32[1,128]{1,0:T(1,128)S(1)} %get-tuple-element.17), channel_id=1, source_target_pairs={{0,4},{4,8},{8,12},{12,16},{16,20},{20,24},{24,28},{1,5},{5,9},{9,... | collective-permute-start | bytes 1544 | tf_op jit(solution)/shard_map/ppermute | solution.py:19
  14.8 11.0 %collective-permute-start.2 = (f32[1,128]{1,0:T(1,128)S(1)}, f32[1,128]{1,0:T(1,128)S(1)}, u32[]{:S(2)}, u32[]{:S(2)}) collective-permute-start(f32[1,128]{1,0:T(1,128)S(1)} %get-tuple-element.18), channel_id=1, source_target_pairs={{4,0},{8,4},{12,8},{16,12},{20,16},{24,20},{28,24},{5,1},{9,5},{13... | collective-permute-start | bytes 1544 | tf_op jit(solution)/shard_map/ppermute | solution.py:21
  19.9 6.0 %collective-permute-start.1 = (f32[2,16,1,128]{3,2,1,0:T(1,128)S(1)}, f32[2,16,1,128]{3,2,1,0:T(1,128)S(1)}, u32[]{:S(2)}, u32[]{:S(2)}) collective-permute-start(f32[2,16,1,128]{3,2,1,0:T(1,128)S(1)} %get-tuple-element.11), channel_id=1, source_target_pairs={{0,4},{4,8},{8,12},{12,16},{16,20},{20,24},{24,28},{1,5},{5,9},{9,... | collective-permute-start | bytes 49160 | tf_op jit(solution)/shard_map/ppermute | solution.py:19
  24.5 6.1 %collective-permute-start.3 = (f32[2,16,1,128]{3,2,1,0:T(1,128)S(1)}, f32[2,16,1,128]{3,2,1,0:T(1,128)S(1)}, u32[]{:S(2)}, u32[]{:S(2)}) collective-permute-start(f32[2,16,1,128]{3,2,1,0:T(1,128)S(1)} %get-tuple-element.12), channel_id=1, source_target_pairs={{4,0},{8,4},{12,8},{16,12},{20,16},{24,20},{28,24},{5,1},{9,5},{13... | collective-permute-start | bytes 49160 | tf_op jit(solution)/shard_map/ppermute | solution.py:21
  30.9 6.3 %collective-permute-start.4 = (f32[2,16,1,128]{3,2,1,0:T(1,128)S(1)}, f32[2,16,1,128]{3,2,1,0:T(1,128)S(1)}, u32[]{:S(2)}, u32[]{:S(2)}) collective-permute-start(f32[2,16,1,128]{3,2,1,0:T(1,128)S(1)} %get-tuple-element.9), channel_id=1, source_target_pairs={{0,4},{4,8},{8,12},{12,16},{16,20},{20,24},{24,28},{1,5},{5,9},{9,... | collective-permute-start | bytes 49160 | tf_op jit(solution)/shard_map/ppermute | solution.py:19
  35.7 5.6 %collective-permute-start.5 = (f32[2,16,1,128]{3,2,1,0:T(1,128)S(1)}, f32[2,16,1,128]{3,2,1,0:T(1,128)S(1)}, u32[]{:S(2)}, u32[]{:S(2)}) collective-permute-start(f32[2,16,1,128]{3,2,1,0:T(1,128)S(1)} %get-tuple-element.10), channel_id=1, source_target_pairs={{4,0},{8,4},{12,8},{16,12},{20,16},{24,20},{28,24},{5,1},{9,5},{13... | collective-permute-start | bytes 49160 | tf_op jit(solution)/shard_map/ppermute | solution.py:21
  41.6 4.4 %collective-permute-start.6 = (f32[2,16,1,128]{3,2,1,0:T(1,128)S(1)}, f32[2,16,1,128]{3,2,1,0:T(1,128)S(1)}, u32[]{:S(2)}, u32[]{:S(2)}) collective-permute-start(f32[2,16,1,128]{3,2,1,0:T(1,128)S(1)} %get-tuple-element.7), channel_id=1, source_target_pairs={{0,4},{4,8},{8,12},{12,16},{16,20},{20,24},{24,28},{1,5},{5,9},{9,... | collective-permute-start | bytes 49160 | tf_op jit(solution)/shard_map/ppermute | solution.py:19
  44.5 5.6 %collective-permute-start.7 = (f32[2,16,1,128]{3,2,1,0:T(1,128)S(1)}, f32[2,16,1,128]{3,2,1,0:T(1,128)S(1)}, u32[]{:S(2)}, u32[]{:S(2)}) collective-permute-start(f32[2,16,1,128]{3,2,1,0:T(1,128)S(1)} %get-tuple-element.8), channel_id=1, source_target_pairs={{4,0},{8,4},{12,8},{16,12},{20,16},{24,20},{28,24},{5,1},{9,5},{13... | collective-permute-start | bytes 49160 | tf_op jit(solution)/shard_map/ppermute | solution.py:21
  50.4 6.3 %collective-permute-start.8 = (f32[2,16,1,128]{3,2,1,0:T(1,128)S(1)}, f32[2,16,1,128]{3,2,1,0:T(1,128)S(1)}, u32[]{:S(2)}, u32[]{:S(2)}) collective-permute-start(f32[2,16,1,128]{3,2,1,0:T(1,128)S(1)} %get-tuple-element.5), channel_id=1, source_target_pairs={{0,4},{4,8},{8,12},{12,16},{16,20},{20,24},{24,28},{1,5},{5,9},{9,... | collective-permute-start | bytes 49160 | tf_op jit(solution)/shard_map/ppermute | solution.py:19
  55.3 5.6 %collective-permute-start.9 = (f32[2,16,1,128]{3,2,1,0:T(1,128)S(1)}, f32[2,16,1,128]{3,2,1,0:T(1,128)S(1)}, u32[]{:S(2)}, u32[]{:S(2)}) collective-permute-start(f32[2,16,1,128]{3,2,1,0:T(1,128)S(1)} %get-tuple-element.6), channel_id=1, source_target_pairs={{4,0},{8,4},{12,8},{16,12},{20,16},{24,20},{28,24},{5,1},{9,5},{13... | collective-permute-start | bytes 49160 | tf_op jit(solution)/shard_map/ppermute | solution.py:21
Sparse Core Ops, SparseCore 0:
  70.1 59.7 reduce-scatter.1
where the time goes:
time: 137 us
  waiting for transfers between devices  77.6 us (57%)
  starting transfers between devices  28.5 us (21%)
  between operations  15 us (11%)
  blocking collectives  7.2 us (5%)
  other arithmetic  3.82 us (3%)
  local copies, waits for them, and re-layouts  3.05 us (2%)
  matrix products  1.54 us (1%)
    reduce_scatter x1, waiting for transfers between devices, per_device(): return lax.psum_scatter(terms, 'tile', scatter_dimension=1, tiled=True)  59.9 us
    ppermute x5, starting transfers between devices, padded_2(): lax.ppermute(tail, axis, [(i, (i + 1) % count) for i in range(ends)])  22 us
    ppermute x5, waiting for transfers between devices, padded_2(): lax.ppermute(head, axis, [((i + 1) % count, i) for i in range(ends)])  17.3 us
    all_gather x1, blocking collectives, per_device(): rows_piece = lax.all_gather(smoothed, 'rows', axis=1, tiled=True)  7.2 us
    ppermute x5, starting transfers between devices, padded_2(): lax.ppermute(head, axis, [((i + 1) % count, i) for i in range(ends)])  6.46 us
  transfers between devices with their start and end apart: 11, of which 8 were waited for; matrix products, arithmetic and copies ran while one was open for 3% of the time, Pallas kernels for 0%

commit v1 on v0

v1 whole, which is shorter than its diff:
```python
import math

import jax
import jax.numpy as jnp
from jax import lax
from jax.sharding import PartitionSpec as P

SMOOTH = 4


def halo_exchange(block, width):
    count = lax.axis_size("tile")
    head = lax.slice_in_dim(block, 0, width, axis=1)
    tail = lax.slice_in_dim(block, block.shape[1] - width, block.shape[1], axis=1)
    from_below = lax.ppermute(tail, "tile", [(i, i + 1) for i in range(count - 1)])
    from_above = lax.ppermute(head, "tile", [(i + 1, i) for i in range(count - 1)])
    return jnp.concatenate([from_below, block, from_above], axis=1)


def step_core(padded, coef_pad):
    middle = padded[..., 1:-1, :]
    coef_mid = coef_pad[1:-1, :]
    face_up = 0.5 * (coef_pad[:-2, :] + coef_mid)
    face_down = 0.5 * (coef_pad[2:, :] + coef_mid)
    side_vals = jnp.pad(middle, [(0, 0)] * (middle.ndim - 1) + [(1, 1)])
    side_coef = jnp.pad(coef_mid, ((0, 0), (1, 1)))
    face_left = 0.5 * (side_coef[:, :-2] + coef_mid)
    face_right = 0.5 * (side_coef[:, 2:] + coef_mid)
    result = middle + face_up * (padded[..., :-2, :] - middle)
    result = result + face_down * (padded[..., 2:, :] - middle)
    result = result + face_left * (side_vals[..., :-2] - middle)
    return result + face_right * (side_vals[..., 2:] - middle)


def per_device(adjoint_rows, panel_index, coef_class, class_gain, cell_coef):
    resident = adjoint_rows.shape[0]
    lines = cell_coef.shape[0]
    cells = cell_coef.shape[1]
    panel_count = panel_index.shape[0]
    per_block = panel_index.shape[1]
    tiles = lax.axis_size("tile")
    halo = SMOOTH
    assert lines >= halo
    classes = jnp.arange(class_gain.shape[0], dtype=jnp.int32)
    own_gain = jnp.sum(jnp.where(classes == coef_class[0], class_gain, 0.0))
    diffusivity = 0.2 * own_gain * cell_coef
    picked = jnp.take(adjoint_rows, panel_index.reshape(-1), axis=0)
    picked = picked.astype(jnp.float32)
    stacked = jnp.concatenate([picked, diffusivity[None]], axis=0)
    wide = halo_exchange(stacked, halo)
    state = wide[:-1]
    coef_wide = wide[-1]
    ext = lines + 2 * halo
    first = lax.axis_index("tile") * lines - halo
    line_no = first + lax.broadcasted_iota(jnp.int32, (ext, 1), 0)
    inside = (line_no >= 0) & (line_no < tiles * lines)
    coef_pad = jnp.pad(coef_wide, ((1, 1), (0, 0)))
    for sweep_no in range(SMOOTH):
        padded = jnp.pad(state, ((0, 0), (1, 1), (0, 0)))
        state = jnp.where(inside[None], step_core(padded, coef_pad), 0.0)
    state = state[:, halo : halo + lines]
    smoothed = state.astype(jnp.bfloat16).reshape(panel_count, per_block, lines, cells)
    flat_rows = adjoint_rows.reshape(resident, lines * cells)
    gram_scale = 1.0 / math.sqrt(tiles * lines * cells)
    rows_piece = lax.all_gather(smoothed, "rows", axis=1, tiled=True)
    panel = rows_piece.shape[1]
    flat_piece = rows_piece.reshape(-1, lines * cells)
    product = lax.dot_general(
        flat_piece, flat_rows, (((1,), (1,)), ((), ())), preferred_element_type=jnp.float32
    )
    terms = (product * gram_scale).reshape(panel_count, tiles, panel // tiles, resident)
    terms = terms.transpose(1, 0, 2, 3)
    parts = lax.all_to_all(terms, "tile", 0, 0, tiled=True)
    return jnp.sum(parts, axis=0)


def solution(mesh):
    return jax.shard_map(
        per_device,
        mesh=mesh,
        in_specs=(P("rows", "tile", None), P(None, "rows"), P("tile"), P(), P("tile", None)),
        out_specs=P(None, "tile", "rows"),
        check_vma=False,
    )
```

time: 137 us -> 43.9 us (0.32)
  waiting for transfers between devices: 77.6 us -> 4.79 us
  starting transfers between devices: 28.5 us -> 6.14 us
  blocking collectives: 7.2 us -> 22.3 us
  between operations: 15 us -> 1.37 us
    reduce_scatter x1 -> x0, waiting for transfers between devices: 59.9 us -> none  [per_device(): return lax.psum_scatter(terms, 'tile', scatter_dimension=1, tiled=True)]
    ppermute x10 -> x2, starting transfers between devices: 28.5 us -> 6.14 us  [the longest x1 4.85 us: halo_exchange(): lax.ppermute(tail, 'tile', [(i, i + 1) for i in range(count - 1)])]
    all_to_all x0 -> x1, blocking collectives: none -> 15 us  [per_device(): parts = lax.all_to_all(terms, 'tile', 0, 0, tiled=True)]
    ppermute x10 -> x2, waiting for transfers between devices: 17.7 us -> 4.79 us  [the longest x1 4.28 us: halo_exchange(): lax.ppermute(head, 'tile', [(i + 1, i) for i in range(count - 1)])]
  transfers between devices with their start and end apart: 11 -> 2, of which waited for: 8 -> 2; matrix products, arithmetic and copies ran while one was open for 3% -> 0% of each run, Pallas kernels for 0% -> 0%
where the time goes in v1:
time: 43.9 us; the launch traced here: 43.6 us
  blocking collectives  22.3 us (51%)
  starting transfers between devices  6.14 us (14%)
  waiting for transfers between devices  4.79 us (11%)
  other arithmetic  4.29 us (10%)
  local copies, waits for them, and re-layouts  3.84 us (9%)
  between operations  1.37 us (3%)
  matrix products  0.83 us (2%)
    all_to_all x1, blocking collectives, per_device(): parts = lax.all_to_all(terms, 'tile', 0, 0, tiled=True)  15 us
    all_gather x1, blocking collectives, per_device(): rows_piece = lax.all_gather(smoothed, 'rows', axis=1, tiled=True)  7.33 us
    ppermute x1, starting transfers between devices, halo_exchange(): lax.ppermute(tail, 'tile', [(i, i + 1) for i in range(count - 1)])  4.85 us
    ppermute x1, waiting for transfers between devices, halo_exchange(): lax.ppermute(head, 'tile', [(i + 1, i) for i in range(count - 1)])  4.28 us
    gather x1, local copies, waits for them, and re-layouts, per_device(): picked = jnp.take(adjoint_rows, panel_index.reshape(-1), axis=0)  2.18 us
    reshape x2, local copies, waits for them, and re-layouts, per_device(): picked = jnp.take(adjoint_rows, panel_index.reshape(-1), axis=0)  1.52 us
    ppermute x1, starting transfers between devices, halo_exchange(): lax.ppermute(head, 'tile', [(i + 1, i) for i in range(count - 1)])  1.29 us
    reduce_sum x1, other arithmetic, per_device(): own_gain = jnp.sum(jnp.where(classes == coef_class[0], class_gain, 0.0))  1.26 us
  transfers between devices with their start and end apart: 2, of which 2 were waited for; matrix products, arithmetic and copies ran while one was open for 0% of the time, Pallas kernels for 0%

profile of v1, /device:TPU:0, one launch (start us, length us, event | category | flops | bytes accessed | tf_op | source)
XLA Modules:
  0.0 43.6 jit_solution(4894000667951856214)
XLA Ops:
  0.0 0.8 %reshape.68 = s32[32,1]{0,1:T(1,128)S(1)} reshape(s32[2,16]{1,0:T(2,128)} %param.6) | data formatting | bytes 256 | tf_op jit(solution)/shard_map/reshape | solution.py:47
  0.8 0.8 %reshape.67 = s32[32]{0:T(128)S(1)} reshape(s32[2,16]{1,0:T(2,128)} %param.6) | data formatting | bytes 256 | tf_op jit(solution)/shard_map/reshape | solution.py:47
  2.2 1.3 %fusion.65 = f32[]{:T(128)} fusion(f32[8]{0:T(128)} %param.8, s32[]{:T(128)} %bitcast.23), kind=kLoop, calls=%fused_computation.101 | loop fusion | flops 23 | bytes 40 | tf_op jit(solution)/shard_map/reduce_sum | solution.py:45
  4.0 0.7 %multiply_bitcast_fusion = f32[1,16,128]{2,1,0:T(8,128)S(1)} fusion(f32[16,128]{1,0:T(8,128)} %param.9, f32[]{:T(128)S(6)} %mul_shard_map.3), kind=kLoop, calls=%fused_computation.94 | loop fusion | flops 2048 | bytes 16388 | tf_op jit(solution)/shard_map/broadcast_in_dim | solution.py:49
  4.7 2.2 %gather_fusion = bf16[32,16,128]{2,1,0:T(8,128)(2,1)S(1)} fusion(bf16[512,16,128]{2,1,0:T(8,128)(2,1)} %param.5, s32[1024]{0:T(1024)S(1)} %pad_clamp_fusion), kind=kCustom, calls=%fused_computation | custom fusion | bytes 262272 | tf_op jit(solution)/shard_map/jit(_take)/gather | solution.py:47
  6.9 0.1 select_convert_fusion
  7.1 4.8 %collective-permute-start = (f32[33,4,128]{2,1,0:T(4,128)S(1)}, f32[33,4,128]{2,1,0:T(4,128)S(1)}, u32[]{:S(2)}, u32[]{:S(2)}) collective-permute-start(f32[33,4,128]{2,1,0:T(4,128)S(1)} %get-tuple-element.9), channel_id=1, source_target_pairs={{0,4},{4,8},{8,12},{12,16},{16,20},{20,24},{24,28},{1,5},{5,9},{9,... | collective-permute-start | bytes 202760 | tf_op jit(solution)/shard_map/ppermute | solution.py:15
  11.9 1.3 %collective-permute-start.1 = (f32[33,4,128]{2,1,0:T(4,128)S(1)}, f32[33,4,128]{2,1,0:T(4,128)S(1)}, u32[]{:S(2)}, u32[]{:S(2)}) collective-permute-start(f32[33,4,128]{2,1,0:T(4,128)S(1)} %get-tuple-element.10), channel_id=1, source_target_pairs={{4,0},{8,4},{12,8},{16,12},{20,16},{24,20},{28,24},{5,1},{9,5},{13... | collective-permute-start | bytes 202760 | tf_op jit(solution)/shard_map/ppermute | solution.py:16
  13.2 0.1 slice.132
  13.3 0.5 %collective-permute-done = f32[33,4,128]{2,1,0:T(4,128)S(1)} collective-permute-done((f32[33,4,128]{2,1,0:T(4,128)S(1)}, f32[33,4,128]{2,1,0:T(4,128)S(1)}, u32[]{:S(2)}, u32[]{:S(2)}) %collective-permute-start) | collective-permute-done | bytes 67616 | tf_op jit(solution)/shard_map/ppermute | solution.py:15
  13.8 4.3 %collective-permute-done.1 = f32[33,4,128]{2,1,0:T(4,128)S(1)} collective-permute-done((f32[33,4,128]{2,1,0:T(4,128)S(1)}, f32[33,4,128]{2,1,0:T(4,128)S(1)}, u32[]{:S(2)}, u32[]{:S(2)}) %collective-permute-start.1) | collective-permute-done | bytes 67616 | tf_op jit(solution)/shard_map/ppermute | solution.py:16
  18.1 0.1 pad_maximum_fusion
  18.2 0.1 fusion.58
  18.3 0.3 fusion.14
  18.6 0.3 fusion.23
  18.9 0.3 fusion.32
  19.2 0.0 copy-start
  19.3 0.3 fusion.36
  19.6 0.2 fusion.53
  19.7 7.3 %all_gather.3 = bf16[2,64,16,128]{3,2,1,0:T(8,128)(2,1)S(1)} all-gather(bf16[2,16,16,128]{3,2,1,0:T(8,128)(2,1)S(1)} %bitcast.26), channel_id=1, replica_groups=mesh['tile'=8,'rows'=4] {'rows'}, dimensions={1}, use_global_device_ids=true | all-gather | bytes 655360 | tf_op jit(solution)/shard_map/all_gather | solution.py:65
  27.1 0.0 copy-done
  27.1 0.8 %fusion.3 = f32[128,512]{1,0:T(8,128)S(1)} fusion(bf16[64,8,16,128]{3,2,1,0:T(8,128)(2,1)S(1)} %bitcast.28, bf16[16,8,16,128]{3,2,1,0:T(8,128)(2,1)S(1)} %bitcast.25), kind=kOutput, calls=%fused_computation.4 | convolution fusion | flops 268500992 | bytes 2883584 | tf_op jit(solution)/shard_map/dot_general | solution.py:68
  28.0 15.0 %all_to_all.5 = f32[8,2,8,512]{3,2,1,0:T(8,128)S(1)} all-to-all(f32[8,2,8,512]{3,2,1,0:T(8,128)S(1)} %bitcast.24), channel_id=1, replica_groups=mesh['tile'=8,'rows'=4] {'tile'}, dimensions={0} | all-to-all | bytes 524288 | tf_op jit(solution)/shard_map/all_to_all | solution.py:73
  42.9 0.6 %reduce_sum.19 = f32[2,8,512]{2,1,0:T(8,128)} reduce(f32[8,2,8,512]{3,2,1,0:T(8,128)S(1)} %all_to_all.5, f32[]{:T(128)} %constant.36.clone.1), dimensions={0}, to_apply=%region_1.2 | reduce | flops 57344 | bytes 294916 | tf_op jit(solution)/shard_map/reduce_sum | solution.py:74
  (11 shorter events, 0.1 us)
Async XLA Ops:
  7.1 6.8 %collective-permute-start = (f32[33,4,128]{2,1,0:T(4,128)S(1)}, f32[33,4,128]{2,1,0:T(4,128)S(1)}, u32[]{:S(2)}, u32[]{:S(2)}) collective-permute-start(f32[33,4,128]{2,1,0:T(4,128)S(1)} %get-tuple-element.9), channel_id=1, source_target_pairs={{0,4},{4,8},{8,12},{12,16},{16,20},{20,24},{24,28},{1,5},{5,9},{9,... | collective-permute-start | bytes 202760 | tf_op jit(solution)/shard_map/ppermute | solution.py:15
  11.9 6.2 %collective-permute-start.1 = (f32[33,4,128]{2,1,0:T(4,128)S(1)}, f32[33,4,128]{2,1,0:T(4,128)S(1)}, u32[]{:S(2)}, u32[]{:S(2)}) collective-permute-start(f32[33,4,128]{2,1,0:T(4,128)S(1)} %get-tuple-element.10), channel_id=1, source_target_pairs={{4,0},{8,4},{12,8},{16,12},{20,16},{24,20},{28,24},{5,1},{9,5},{13... | collective-permute-start | bytes 202760 | tf_op jit(solution)/shard_map/ppermute | solution.py:16
  19.2 7.8 %copy-start = (bf16[512,16,128]{2,1,0:T(8,128)(2,1)S(1)}, bf16[512,16,128]{2,1,0:T(8,128)(2,1)}, u32[]{:S(2)}) copy-start(bf16[512,16,128]{2,1,0:T(8,128)(2,1)} %param.5) | copy-start | bytes 6291460

commit v2 on v1

--- a/solution.py
+++ b/solution.py
@@ -6,15 +6,6 @@
 from jax.sharding import PartitionSpec as P
 
 SMOOTH = 4
-
-
-def halo_exchange(block, width):
-    count = lax.axis_size("tile")
-    head = lax.slice_in_dim(block, 0, width, axis=1)
-    tail = lax.slice_in_dim(block, block.shape[1] - width, block.shape[1], axis=1)
-    from_below = lax.ppermute(tail, "tile", [(i, i + 1) for i in range(count - 1)])
-    from_above = lax.ppermute(head, "tile", [(i + 1, i) for i in range(count - 1)])
-    return jnp.concatenate([from_below, block, from_above], axis=1)
 
 
 def step_core(padded, coef_pad):
@@ -41,15 +32,34 @@
     tiles = lax.axis_size("tile")
     halo = SMOOTH
     assert lines >= halo
-    classes = jnp.arange(class_gain.shape[0], dtype=jnp.int32)
-    own_gain = jnp.sum(jnp.where(classes == coef_class[0], class_gain, 0.0))
-    diffusivity = 0.2 * own_gain * cell_coef
-    picked = jnp.take(adjoint_rows, panel_index.reshape(-1), axis=0)
-    picked = picked.astype(jnp.float32)
-    stacked = jnp.concatenate([picked, diffusivity[None]], axis=0)
-    wide = halo_exchange(stacked, halo)
-    state = wide[:-1]
-    coef_wide = wide[-1]
+    lo_rows = adjoint_rows[:, :halo].at[panel_index].get(mode="promise_in_bounds")
+    hi_rows = adjoint_rows[:, lines - halo :].at[panel_index].get(mode="promise_in_bounds")
+    own_class = jnp.broadcast_to(coef_class.astype(jnp.float32).reshape(1, 1, 1), (1, halo, cells))
+
+    def edge(rows, coef):
+        flat = rows.reshape(-1, halo, cells).astype(jnp.float32)
+        return jnp.concatenate([flat, coef[None], own_class], axis=0)
+
+    count = lax.axis_size("tile")
+    from_below = lax.ppermute(edge(hi_rows, cell_coef[lines - halo :]), "tile", [(i, i + 1) for i in range(count - 1)])
+    from_above = lax.ppermute(edge(lo_rows, cell_coef[:halo]), "tile", [(i + 1, i) for i in range(count - 1)])
+
+    def diffusion(raw_coef, class_code):
+        gain = class_gain[class_code]
+        return 0.2 * gain * raw_coef
+
+    diffusivity = diffusion(cell_coef, coef_class[0])
+    picked = adjoint_rows.at[panel_index].get(mode="promise_in_bounds")
+    picked = picked.reshape(-1, lines, cells).astype(jnp.float32)
+    state = jnp.concatenate([from_below[:-2], picked, from_above[:-2]], axis=1)
+    coef_wide = jnp.concatenate(
+        [
+            diffusion(from_below[-2], from_below[-1, 0, 0].astype(jnp.int32)),
+            diffusivity,
+            diffusion(from_above[-2], from_above[-1, 0, 0].astype(jnp.int32)),
+        ],
+        axis=0,
+    )
     ext = lines + 2 * halo
     first = lax.axis_index("tile") * lines - halo
     line_no = first + lax.broadcasted_iota(jnp.int32, (ext, 1), 0)

time: 43.9 us -> 46.2 us (1.052)
  between operations: 1.37 us -> 4.24 us
  local copies, waits for them, and re-layouts: 3.84 us -> 6.44 us
  waiting for transfers between devices: 4.79 us -> 2.99 us
  other arithmetic: 4.29 us -> 3.02 us
    slice x1 -> x5, local copies, waits for them, and re-layouts: 0.03 us -> 2.98 us  [the longest x1 1.95 us: per_device(): adjoint_rows[:, lines - halo:].at[panel_index].get(mode='promise_in_bounds')]
    ppermute x2, waiting for transfers between devices: 4.79 us -> 2.99 us  [the longest x1 2.99 us: per_device(): lax.ppermute(edge(lo_rows, cell_coef[:halo]), 'tile', [(i + 1, i) for i i...]
    reshape x2 -> x0, local copies, waits for them, and re-layouts: 1.52 us -> none  [per_device(): picked = jnp.take(adjoint_rows, panel_index.reshape(-1), axis=0)]
    reduce_sum x1 -> x0, other arithmetic: 1.26 us -> none  [per_device(): own_gain = jnp.sum(jnp.where(classes == coef_class[0], class_gain, 0.0))]
    broadcast_in_dim x0 -> x2, local copies, waits for them, and re-layouts: none -> 0.79 us  [the longest x1 0.71 us: edge(): return jnp.concatenate([flat, coef[None], own_class], axis=0)]
    broadcast_in_dim x1 -> x0, other arithmetic: 0.7 us -> none  [per_device(): stacked = jnp.concatenate([picked, diffusivity[None]], axis=0)]
    select_n x1, other arithmetic: 0.01 us -> 0.68 us  [per_device(): adjoint_rows[:, lines - halo:].at[panel_index].get(mode='promise_in_bounds')]
    dynamic_slice x0 -> x1, local copies, waits for them, and re-layouts: none -> 0.66 us  [diffusion(): gain = class_gain[class_code]]
  transfers between devices with their start and end apart: 2 -> 2, of which waited for: 2 -> 1; matrix products, arithmetic and copies ran while one was open for 0% -> 3% of each run, Pallas kernels for 0% -> 0%
where the time goes in v2:
time: 46.2 us; the launch traced here: 45.8 us
  blocking collectives  22.2 us (48%)
  local copies, waits for them, and re-layouts  6.44 us (14%)
  starting transfers between devices  6.14 us (13%)
  between operations  4.24 us (9%)
  other arithmetic  3.02 us (7%)
  waiting for transfers between devices  2.99 us (6%)
  matrix products  0.83 us (2%)
    all_to_all x1, blocking collectives, per_device(): parts = lax.all_to_all(terms, 'tile', 0, 0, tiled=True)  15 us
    all_gather x1, blocking collectives, per_device(): rows_piece = lax.all_gather(smoothed, 'rows', axis=1, tiled=True)  7.2 us
    ppermute x1, starting transfers between devices, per_device(): lax.ppermute(edge(hi_rows, cell_coef[lines - halo:]), 'tile', [(i, i + 1)...  4.85 us
    ppermute x1, waiting for transfers between devices, per_device(): lax.ppermute(edge(lo_rows, cell_coef[:halo]), 'tile', [(i + 1, i) for i i...  2.99 us
    slice x1, local copies, waits for them, and re-layouts, per_device(): adjoint_rows[:, lines - halo:].at[panel_index].get(mode='promise_in_bounds')  1.95 us
    ppermute x1, starting transfers between devices, per_device(): lax.ppermute(edge(lo_rows, cell_coef[:halo]), 'tile', [(i + 1, i) for i i...  1.29 us
  transfers between devices with their start and end apart: 2, of which 1 were waited for; matrix products, arithmetic and copies ran while one was open for 3% of the time, Pallas kernels for 0%

profile of v2, /device:TPU:0, one launch (start us, length us, event | category | flops | bytes accessed | tf_op | source)
XLA Modules:
  0.0 45.8 jit_solution(6952712198727744681)
XLA Ops:
  0.0 0.0 copy-start.1
  0.8 0.7 %compare_select_fusion = s32[2,16]{1,0:T(2,128)S(1)} fusion(s32[2,16]{1,0:T(2,128)} %param.6), kind=kLoop, calls=%fused_computation.97 | loop fusion | flops 96 | bytes 256 | tf_op jit(solution)/shard_map/select_n | solution.py:36
  1.5 0.1 reshape.62
  1.6 0.7 %slice_bitcast_fusion.1 = (f32[1,4,128]{2,1,0:T(4,128)S(1)}, f32[1,4,128]{2,1,0:T(4,128)S(1)}) fusion(f32[16,128]{1,0:T(8,128)} %param.9), kind=kLoop, calls=%fused_computation.103 | loop fusion | bytes 8192 | tf_op jit(solution)/shard_map/broadcast_in_dim | solution.py:41
  2.3 1.9 %fusion.67 = (bf16[512,4,128]{2,1,0:T(4,128)(2,1)S(1)}, bf16[512,4,128]{2,1,0:T(4,128)(2,1)S(1)}) fusion(bf16[512,16,128]{2,1,0:T(8,128)(2,1)} %param.5), kind=kLoop, calls=%fused_computation.105 | loop fusion | bytes 2097152 | tf_op jit(solution)/shard_map/slice | solution.py:36
  4.2 0.6 %gather_fusion = bf16[32,4,128]{2,1,0:T(4,128)(2,1)S(1)} fusion(bf16[512,4,128]{2,1,0:T(4,128)(2,1)S(1)} %get-tuple-element.5, s32[1024]{0:T(1024)S(1)} %pad_clamp_fusion), kind=kCustom, calls=%fused_computation | custom fusion | bytes 65664 | tf_op jit(solution)/shard_map/gather | solution.py:36
  4.9 0.6 %gather_fusion.2 = bf16[32,4,128]{2,1,0:T(4,128)(2,1)S(1)} fusion(bf16[512,4,128]{2,1,0:T(4,128)(2,1)S(1)} %get-tuple-element.6, s32[1024]{0:T(1024)S(1)} %pad_clamp_fusion), kind=kCustom, calls=%fused_computation.2 | custom fusion | bytes 65664 | tf_op jit(solution)/shard_map/gather | solution.py:35
  5.5 0.1 pad.58.clone
  5.6 0.1 maximum_maximum_fusion
  5.7 4.8 %collective-permute-start = (f32[34,4,128]{2,1,0:T(4,128)S(1)}, f32[34,4,128]{2,1,0:T(4,128)S(1)}, u32[]{:S(2)}, u32[]{:S(2)}) collective-permute-start(f32[34,4,128]{2,1,0:T(4,128)S(1)} %get-tuple-element.20), channel_id=1, source_target_pairs={{0,4},{4,8},{8,12},{12,16},{16,20},{20,24},{24,28},{1,5},{5,9},{9,... | collective-permute-start | bytes 208904 | tf_op jit(solution)/shard_map/ppermute | solution.py:44
  10.5 1.3 %collective-permute-start.1 = (f32[34,4,128]{2,1,0:T(4,128)S(1)}, f32[34,4,128]{2,1,0:T(4,128)S(1)}, u32[]{:S(2)}, u32[]{:S(2)}) collective-permute-start(f32[34,4,128]{2,1,0:T(4,128)S(1)} %get-tuple-element.21), channel_id=1, source_target_pairs={{4,0},{8,4},{12,8},{16,12},{20,16},{24,20},{28,24},{5,1},{9,5},{13... | collective-permute-start | bytes 208904 | tf_op jit(solution)/shard_map/ppermute | solution.py:45
  11.8 0.0 copy-done
  11.9 0.6 %gather_fusion.1 = bf16[32,16,128]{2,1,0:T(8,128)(2,1)S(1)} fusion(bf16[512,16,128]{2,1,0:T(8,128)(2,1)S(1)} %copy-done, s32[1024]{0:T(1024)S(1)} %pad_clamp_fusion), kind=kCustom, calls=%fused_computation.1 | custom fusion | bytes 262272 | tf_op jit(solution)/shard_map/gather | solution.py:52
  12.5 0.1 slice.165
  12.6 0.0 collective-permute-done
  12.6 0.5 %slice.153 = f32[1,1,1]{2,1,0:T(1,128)} slice(f32[34,4,128]{2,1,0:T(4,128)S(1)} %collective-permute-done), slice={[33:34], [0:1], [0:1]} | slice | bytes 8 | tf_op jit(solution)/shard_map/slice | solution.py:57
  13.8 3.0 %collective-permute-done.1 = f32[34,4,128]{2,1,0:T(4,128)S(1)} collective-permute-done((f32[34,4,128]{2,1,0:T(4,128)S(1)}, f32[34,4,128]{2,1,0:T(4,128)S(1)}, u32[]{:S(2)}, u32[]{:S(2)}) %collective-permute-start.1) | collective-permute-done | bytes 69664 | tf_op jit(solution)/shard_map/ppermute | solution.py:45
  16.7 0.5 %slice.155 = f32[1,1,1]{2,1,0:T(1,128)} slice(f32[34,4,128]{2,1,0:T(4,128)S(1)} %collective-permute-done.1), slice={[33:34], [0:1], [0:1]} | slice | bytes 8 | tf_op jit(solution)/shard_map/slice | solution.py:59
  17.9 0.0 copy-done.2
  17.9 0.7 %fusion.68 = (f32[1]{0:T(128)}, f32[1]{0:T(128)}, f32[1]{0:T(128)}) fusion(f32[8]{0:T(128)S(1)} %copy-done.2, s32[]{:T(128)S(6)} %select_n.28, s32[]{:T(128)S(6)} %select_n.30, s32[]{:T(128)S(6)} %select_n.29), kind=kLoop, calls=%fused_computation.106 | loop fusion | bytes 36 | tf_op jit(solution)/shard_map/dynamic_slice | solution.py:48
  20.5 0.0 copy-done.1
  20.5 0.1 fusion.58
  20.7 0.1 pad_maximum_fusion
  20.7 0.3 fusion.14
  21.0 0.3 fusion.23
  21.4 0.3 fusion.32
  21.7 0.3 fusion.36
  22.0 0.2 fusion.53
  22.2 7.2 %all_gather.3 = bf16[2,64,16,128]{3,2,1,0:T(8,128)(2,1)S(1)} all-gather(bf16[2,16,16,128]{3,2,1,0:T(8,128)(2,1)S(1)} %bitcast.37), channel_id=1, replica_groups=mesh['tile'=8,'rows'=4] {'rows'}, dimensions={1}, use_global_device_ids=true | all-gather | bytes 655360 | tf_op jit(solution)/shard_map/all_gather | solution.py:75
  29.4 0.8 %fusion.3 = f32[128,512]{1,0:T(8,128)S(1)} fusion(bf16[64,8,16,128]{3,2,1,0:T(8,128)(2,1)S(1)} %bitcast.35, bf16[16,8,16,128]{3,2,1,0:T(8,128)(2,1)S(1)} %bitcast.36), kind=kOutput, calls=%fused_computation.6 | convolution fusion | flops 268500992 | bytes 2883584 | tf_op jit(solution)/shard_map/dot_general | solution.py:78
  30.2 15.0 %all_to_all.5 = f32[8,2,8,512]{3,2,1,0:T(8,128)S(1)} all-to-all(f32[8,2,8,512]{3,2,1,0:T(8,128)S(1)} %bitcast.34), channel_id=1, replica_groups=mesh['tile'=8,'rows'=4] {'tile'}, dimensions={0} | all-to-all | bytes 524288 | tf_op jit(solution)/shard_map/all_to_all | solution.py:83
  45.2 0.6 %reduce_sum.9 = f32[2,8,512]{2,1,0:T(8,128)} reduce(f32[8,2,8,512]{3,2,1,0:T(8,128)S(1)} %all_to_all.5, f32[]{:T(128)} %constant.30.clone.1), dimensions={0}, to_apply=%region_0.1 | reduce | flops 57344 | bytes 294916 | tf_op jit(solution)/shard_map/reduce_sum | solution.py:84
  (16 shorter events, 0.1 us)
Async XLA Ops:
  0.0 20.5 %copy-start.1 = (f32[16,128]{1,0:T(8,128)S(1)}, f32[16,128]{1,0:T(8,128)}, u32[]{:S(2)}) copy-start(f32[16,128]{1,0:T(8,128)} %param.9) | copy-start | bytes 24580
  0.0 11.8 %copy-start = (bf16[512,16,128]{2,1,0:T(8,128)(2,1)S(1)}, bf16[512,16,128]{2,1,0:T(8,128)(2,1)}, u32[]{:S(2)}) copy-start(bf16[512,16,128]{2,1,0:T(8,128)(2,1)} %param.5) | copy-start | bytes 6291460
  0.0 17.9 %copy-start.2 = (f32[8]{0:T(128)S(1)}, f32[8]{0:T(128)}, u32[]{:S(2)}) copy-start(f32[8]{0:T(128)} %param.8) | copy-start | bytes 100
  5.7 6.9 %collective-permute-start = (f32[34,4,128]{2,1,0:T(4,128)S(1)}, f32[34,4,128]{2,1,0:T(4,128)S(1)}, u32[]{:S(2)}, u32[]{:S(2)}) collective-permute-start(f32[34,4,128]{2,1,0:T(4,128)S(1)} %get-tuple-element.20), channel_id=1, source_target_pairs={{0,4},{4,8},{8,12},{12,16},{16,20},{20,24},{24,28},{1,5},{5,9},{9,... | collective-permute-start | bytes 208904 | tf_op jit(solution)/shard_map/ppermute | solution.py:44
  10.5 6.2 %collective-permute-start.1 = (f32[34,4,128]{2,1,0:T(4,128)S(1)}, f32[34,4,128]{2,1,0:T(4,128)S(1)}, u32[]{:S(2)}, u32[]{:S(2)}) collective-permute-start(f32[34,4,128]{2,1,0:T(4,128)S(1)} %get-tuple-element.21), channel_id=1, source_target_pairs={{4,0},{8,4},{12,8},{16,12},{20,16},{24,20},{28,24},{5,1},{9,5},{13... | collective-permute-start | bytes 208904 | tf_op jit(solution)/shard_map/ppermute | solution.py:45

commit v3 on v2

--- a/solution.py
+++ b/solution.py
@@ -32,33 +32,37 @@
     tiles = lax.axis_size("tile")
     halo = SMOOTH
     assert lines >= halo
-    lo_rows = adjoint_rows[:, :halo].at[panel_index].get(mode="promise_in_bounds")
-    hi_rows = adjoint_rows[:, lines - halo :].at[panel_index].get(mode="promise_in_bounds")
+    picked = lax.gather(
+        adjoint_rows,
+        panel_index[..., None],
+        lax.GatherDimensionNumbers(offset_dims=(2, 3), collapsed_slice_dims=(0,), start_index_map=(0,)),
+        (1, lines, cells),
+        mode=lax.GatherScatterMode.PROMISE_IN_BOUNDS,
+    )
+    picked = picked.reshape(-1, lines, cells).astype(jnp.float32)
+    edge_rows = jnp.concatenate([picked[:, :halo], picked[:, lines - halo :]], axis=0)
+    flat_index = panel_index.reshape(-1, 1)
+    picks = flat_index.shape[0]
     own_class = jnp.broadcast_to(coef_class.astype(jnp.float32).reshape(1, 1, 1), (1, halo, cells))
 
     def edge(rows, coef):
-        flat = rows.reshape(-1, halo, cells).astype(jnp.float32)
-        return jnp.concatenate([flat, coef[None], own_class], axis=0)
+        return jnp.concatenate([rows, coef[None], own_class], axis=0)
 
     count = lax.axis_size("tile")
-    from_below = lax.ppermute(edge(hi_rows, cell_coef[lines - halo :]), "tile", [(i, i + 1) for i in range(count - 1)])
-    from_above = lax.ppermute(edge(lo_rows, cell_coef[:halo]), "tile", [(i + 1, i) for i in range(count - 1)])
+    from_below = lax.ppermute(
+        edge(edge_rows[picks:], cell_coef[lines - halo :]), "tile", [(i, i + 1) for i in range(count - 1)]
+    )
+    from_above = lax.ppermute(edge(edge_rows[:picks], cell_coef[:halo]), "tile", [(i + 1, i) for i in range(count - 1)])
+    classes = lax.broadcasted_iota(jnp.int32, (class_gain.shape[0], 1, 1), 0).astype(jnp.float32)
 
     def diffusion(raw_coef, class_code):
-        gain = class_gain[class_code]
+        gain = jnp.sum(jnp.where(classes == class_code[None], class_gain[:, None, None], 0.0), axis=0)
         return 0.2 * gain * raw_coef
 
-    diffusivity = diffusion(cell_coef, coef_class[0])
-    picked = adjoint_rows.at[panel_index].get(mode="promise_in_bounds")
-    picked = picked.reshape(-1, lines, cells).astype(jnp.float32)
+    diffusivity = diffusion(cell_coef, jnp.broadcast_to(coef_class.astype(jnp.float32)[:, None], cell_coef.shape))
     state = jnp.concatenate([from_below[:-2], picked, from_above[:-2]], axis=1)
     coef_wide = jnp.concatenate(
-        [
-            diffusion(from_below[-2], from_below[-1, 0, 0].astype(jnp.int32)),
-            diffusivity,
-            diffusion(from_above[-2], from_above[-1, 0, 0].astype(jnp.int32)),
-        ],
-        axis=0,
+        [diffusion(from_below[-2], from_below[-1]), diffusivity, diffusion(from_above[-2], from_above[-1])], axis=0
     )
     ext = lines + 2 * halo
     first = lax.axis_index("tile") * lines - halo

time: 46.2 us -> 42.2 us (0.913)
  between operations: 4.24 us -> 0.82 us
  local copies, waits for them, and re-layouts: 6.44 us -> 3.88 us
  other arithmetic: 3.02 us -> 4.51 us
    slice x3 -> x1, local copies, waits for them, and re-layouts: 2.97 us -> 0.02 us  [per_device(): picked[:, lines - halo:]]
    reduce_sum x0 -> x2, other arithmetic: none -> 1.48 us  [diffusion(): jnp.sum(jnp.where(classes == class_code[None], class_gain[:, None, None],...]
    mul x2, other arithmetic: 0.01 us -> 0.71 us  [diffusion(): return 0.2 * gain * raw_coef]
    select_n x1 -> x0, other arithmetic: 0.68 us -> none  [per_device(): adjoint_rows[:, lines - halo:].at[panel_index].get(mode='promise_in_bounds')]
    broadcast_in_dim x2, local copies, waits for them, and re-layouts: 0.79 us -> 1.47 us  [the longest x1 0.76 us: per_device(): panel_index[..., None]]
    dynamic_slice x1 -> x0, local copies, waits for them, and re-layouts: 0.66 us -> none  [diffusion(): gain = class_gain[class_code]]
    gather x3 -> x1, local copies, waits for them, and re-layouts: 1.81 us -> 2.18 us  [per_device(): lax.gather(adjoint_rows, panel_index[..., None], lax.GatherDimensionNumbe...]
  transfers between devices with their start and end apart: 2 -> 2, of which waited for: 1 -> 1; matrix products, arithmetic and copies ran while one was open for 3% -> 4% of each run, Pallas kernels for 0% -> 0%
where the time goes in v3:
time: 42.2 us; the launch traced here: 41.8 us
  blocking collectives  22.3 us (53%)
  starting transfers between devices  6.14 us (15%)
  other arithmetic  4.51 us (11%)
  local copies, waits for them, and re-layouts  3.88 us (9%)
  waiting for transfers between devices  3.31 us (8%)
  matrix products  0.83 us (2%)
  between operations  0.82 us (2%)
    all_to_all x1, blocking collectives, per_device(): parts = lax.all_to_all(terms, 'tile', 0, 0, tiled=True)  15 us
    all_gather x1, blocking collectives, per_device(): rows_piece = lax.all_gather(smoothed, 'rows', axis=1, tiled=True)  7.33 us
    ppermute x1, starting transfers between devices, per_device(): lax.ppermute(edge(edge_rows[picks:], cell_coef[lines - halo:]), 'tile', [...  4.85 us
    ppermute x1, waiting for transfers between devices, per_device(): lax.ppermute(edge(edge_rows[:picks], cell_coef[:halo]), 'tile', [(i + 1,...  3.31 us
    gather x1, local copies, waits for them, and re-layouts, per_device(): lax.gather(adjoint_rows, panel_index[..., None], lax.GatherDimensionNumbe...  2.18 us
    reduce_sum x2, other arithmetic, diffusion(): jnp.sum(jnp.where(classes == class_code[None], class_gain[:, None, None],...  1.48 us
    ppermute x1, starting transfers between devices, per_device(): lax.ppermute(edge(edge_rows[:picks], cell_coef[:halo]), 'tile', [(i + 1,...  1.29 us
    select_n x3, other arithmetic, per_device(): state = jnp.where(inside[None], step_core(padded, coef_pad), 0.0)  0.91 us
  transfers between devices with their start and end apart: 2, of which 1 were waited for; matrix products, arithmetic and copies ran while one was open for 4% of the time, Pallas kernels for 0%

profile of v3, /device:TPU:0, one launch (start us, length us, event | category | flops | bytes accessed | tf_op | source)
XLA Modules:
  0.0 41.8 jit_solution(15100518266434130843)
XLA Ops:
  0.7 0.8 %reshape.49 = s32[32]{0:T(128)S(1)} reshape(s32[2,16]{1,0:T(2,128)} %param.6) | data formatting | bytes 256 | tf_op jit(solution)/shard_map/broadcast_in_dim | solution.py:37
  1.4 0.7 %slice_bitcast_fusion.5 = (f32[1,4,128]{2,1,0:T(4,128)S(1)}, f32[1,4,128]{2,1,0:T(4,128)S(1)}) fusion(f32[16,128]{1,0:T(8,128)} %param.9), kind=kLoop, calls=%fused_computation.105 | loop fusion | bytes 8192 | tf_op jit(solution)/shard_map/broadcast_in_dim | solution.py:49
  2.1 2.2 %gather_fusion = bf16[32,16,128]{2,1,0:T(8,128)(2,1)S(1)} fusion(bf16[512,16,128]{2,1,0:T(8,128)(2,1)} %param.5, s32[1024]{0:T(1024)S(1)} %pad_clamp_fusion), kind=kCustom, calls=%fused_computation | custom fusion | bytes 262272 | tf_op jit(solution)/shard_map/gather | solution.py:35
  4.3 0.1 pad.58.clone
  4.4 0.1 maximum_maximum_fusion
  4.5 4.8 %collective-permute-start = (f32[34,4,128]{2,1,0:T(4,128)S(1)}, f32[34,4,128]{2,1,0:T(4,128)S(1)}, u32[]{:S(2)}, u32[]{:S(2)}) collective-permute-start(f32[34,4,128]{2,1,0:T(4,128)S(1)} %get-tuple-element.19), channel_id=1, source_target_pairs={{0,4},{4,8},{8,12},{12,16},{16,20},{20,24},{24,28},{1,5},{5,9},{9,... | collective-permute-start | bytes 208904 | tf_op jit(solution)/shard_map/ppermute | solution.py:52
  9.4 1.3 %collective-permute-start.1 = (f32[34,4,128]{2,1,0:T(4,128)S(1)}, f32[34,4,128]{2,1,0:T(4,128)S(1)}, u32[]{:S(2)}, u32[]{:S(2)}) collective-permute-start(f32[34,4,128]{2,1,0:T(4,128)S(1)} %get-tuple-element.20), channel_id=1, source_target_pairs={{4,0},{8,4},{12,8},{16,12},{20,16},{24,20},{28,24},{5,1},{9,5},{13... | collective-permute-start | bytes 208904 | tf_op jit(solution)/shard_map/ppermute | solution.py:55
  10.7 0.1 slice.163
  10.8 0.7 %select_reduce_fusion = f32[16,128]{1,0:T(8,128)S(1)} fusion(f32[8]{0:T(128)} %param.8, pred[8]{0:T(512)(128)(4,1)S(1)} %broadcast_compare_fusion), kind=kLoop, calls=%fused_computation.80 | loop fusion | flops 30720 | bytes 8232 | tf_op jit(solution)/shard_map/reduce_sum | solution.py:59
  11.6 0.7 %multiply_multiply_fusion = f32[16,128]{1,0:T(8,128)S(1)} fusion(f32[16,128]{1,0:T(8,128)} %param.9, f32[16,128]{1,0:T(8,128)S(1)} %select_reduce_fusion), kind=kLoop, calls=%fused_computation.96 | loop fusion | flops 4096 | bytes 24576 | tf_op jit(solution)/shard_map/mul | solution.py:60
  12.3 0.0 collective-permute-done
  12.3 3.3 %collective-permute-done.1 = f32[34,4,128]{2,1,0:T(4,128)S(1)} collective-permute-done((f32[34,4,128]{2,1,0:T(4,128)S(1)}, f32[34,4,128]{2,1,0:T(4,128)S(1)}, u32[]{:S(2)}, u32[]{:S(2)}) %collective-permute-start.1) | collective-permute-done | bytes 69664 | tf_op jit(solution)/shard_map/ppermute | solution.py:55
  15.6 0.7 %select_reduce_fusion.2 = (f32[4,128]{1,0:T(4,128)S(1)}, f32[4,128]{1,0:T(4,128)S(1)}) fusion(f32[8]{0:T(128)} %param.8, f32[4,128]{1,0:T(4,128)S(1)} %slice_bitcast_fusion.3, f32[8]{0:T(128)S(1)} %iota_convert_fusion, f32[4,128]{1,0:T(4,128)S(1)} %slice_bitcast_fusion.1), kind=kLoop, calls=%fused_computation.86 | loop fusion | flops 23552 | bytes 8256 | tf_op jit(solution)/shard_map/reduce_sum | solution.py:59
  16.4 0.1 fusion.58
  16.5 0.1 pad_maximum_fusion
  16.6 0.3 fusion.14
  16.9 0.3 fusion.23
  17.2 0.3 fusion.32
  17.5 0.0 copy-start
  17.5 0.3 fusion.36
  17.8 0.2 fusion.53
  18.0 7.3 %all_gather.3 = bf16[2,64,16,128]{3,2,1,0:T(8,128)(2,1)S(1)} all-gather(bf16[2,16,16,128]{3,2,1,0:T(8,128)(2,1)S(1)} %bitcast.35), channel_id=1, replica_groups=mesh['tile'=8,'rows'=4] {'rows'}, dimensions={1}, use_global_device_ids=true | all-gather | bytes 655360 | tf_op jit(solution)/shard_map/all_gather | solution.py:79
  25.3 0.0 copy-done
  25.3 0.8 %fusion.3 = f32[128,512]{1,0:T(8,128)S(1)} fusion(bf16[64,8,16,128]{3,2,1,0:T(8,128)(2,1)S(1)} %bitcast.37, bf16[16,8,16,128]{3,2,1,0:T(8,128)(2,1)S(1)} %bitcast.34), kind=kOutput, calls=%fused_computation.4 | convolution fusion | flops 268500992 | bytes 2883584 | tf_op jit(solution)/shard_map/dot_general | solution.py:82
  26.2 15.0 %all_to_all.5 = f32[8,2,8,512]{3,2,1,0:T(8,128)S(1)} all-to-all(f32[8,2,8,512]{3,2,1,0:T(8,128)S(1)} %bitcast.33), channel_id=1, replica_groups=mesh['tile'=8,'rows'=4] {'tile'}, dimensions={0} | all-to-all | bytes 524288 | tf_op jit(solution)/shard_map/all_to_all | solution.py:87
  41.2 0.6 %reduce_sum.39 = f32[2,8,512]{2,1,0:T(8,128)} reduce(f32[8,2,8,512]{3,2,1,0:T(8,128)S(1)} %all_to_all.5, f32[]{:T(128)} %constant.8.clone.1), dimensions={0}, to_apply=%region_3.4 | reduce | flops 57344 | bytes 294916 | tf_op jit(solution)/shard_map/reduce_sum | solution.py:88
  (16 shorter events, 0.1 us)
Async XLA Ops:
  4.5 7.7 %collective-permute-start = (f32[34,4,128]{2,1,0:T(4,128)S(1)}, f32[34,4,128]{2,1,0:T(4,128)S(1)}, u32[]{:S(2)}, u32[]{:S(2)}) collective-permute-start(f32[34,4,128]{2,1,0:T(4,128)S(1)} %get-tuple-element.19), channel_id=1, source_target_pairs={{0,4},{4,8},{8,12},{12,16},{16,20},{20,24},{24,28},{1,5},{5,9},{9,... | collective-permute-start | bytes 208904 | tf_op jit(solution)/shard_map/ppermute | solution.py:52
  9.4 6.2 %collective-permute-start.1 = (f32[34,4,128]{2,1,0:T(4,128)S(1)}, f32[34,4,128]{2,1,0:T(4,128)S(1)}, u32[]{:S(2)}, u32[]{:S(2)}) collective-permute-start(f32[34,4,128]{2,1,0:T(4,128)S(1)} %get-tuple-element.20), channel_id=1, source_target_pairs={{4,0},{8,4},{12,8},{16,12},{20,16},{24,20},{28,24},{5,1},{9,5},{13... | collective-permute-start | bytes 208904 | tf_op jit(solution)/shard_map/ppermute | solution.py:55
  17.5 7.8 %copy-start = (bf16[512,16,128]{2,1,0:T(8,128)(2,1)S(1)}, bf16[512,16,128]{2,1,0:T(8,128)(2,1)}, u32[]{:S(2)}) copy-start(bf16[512,16,128]{2,1,0:T(8,128)(2,1)} %param.5) | copy-start | bytes 6291460

commit v4 on v3

--- a/solution.py
+++ b/solution.py
@@ -1,11 +1,52 @@
+import functools
 import math
 
 import jax
 import jax.numpy as jnp
 from jax import lax
+from jax.experimental import pallas as pl
+from jax.experimental.pallas import tpu as pltpu
 from jax.sharding import PartitionSpec as P
 
 SMOOTH = 4
+
+
+def gather_kernel(halo, index_ref, class_ref, rows_hbm, coef_ref, picked_ref, down_ref, up_ref, buf, sems):
+    panels, per_block = index_ref.shape
+    count = panels * per_block
+    lines = buf.shape[1]
+    copies = []
+    for i in range(count):
+        copy = pltpu.make_async_copy(rows_hbm.at[index_ref[i // per_block, i % per_block]], buf.at[i], sems.at[i])
+        copy.start()
+        copies.append(copy)
+    for copy in copies:
+        copy.wait()
+    rows = buf[...].astype(jnp.float32)
+    picked_ref[...] = rows
+    code = jnp.full(down_ref.shape[1:], class_ref[0].astype(jnp.float32), jnp.float32)
+    down_ref[:count] = rows[:, :halo]
+    down_ref[count] = coef_ref[:halo]
+    down_ref[count + 1] = code
+    up_ref[:count] = rows[:, lines - halo :]
+    up_ref[count] = coef_ref[lines - halo :]
+    up_ref[count + 1] = code
+
+
+def gather_rows(adjoint_rows, panel_index, coef_class, cell_coef, halo):
+    count = panel_index.size
+    lines, cells = cell_coef.shape
+    edge = jax.ShapeDtypeStruct((count + 2, halo, cells), jnp.float32)
+    smem = pl.BlockSpec(memory_space=pltpu.SMEM)
+    vmem = pl.BlockSpec(memory_space=pltpu.VMEM)
+    return pl.pallas_call(
+        functools.partial(gather_kernel, halo),
+        out_shape=(jax.ShapeDtypeStruct((count, lines, cells), jnp.float32), edge, edge),
+        in_specs=[smem, smem, pl.BlockSpec(memory_space=pl.ANY), vmem],
+        out_specs=(vmem, vmem, vmem),
+        scratch_shapes=[pltpu.VMEM((count, lines, cells), adjoint_rows.dtype), pltpu.SemaphoreType.DMA((count,))],
+        cost_estimate=pl.CostEstimate(flops=0, transcendentals=0, bytes_accessed=count * lines * cells * 6),
+    )(panel_index, coef_class, adjoint_rows, cell_coef)
 
 
 def step_core(padded, coef_pad):
@@ -32,27 +73,10 @@
     tiles = lax.axis_size("tile")
     halo = SMOOTH
     assert lines >= halo
-    picked = lax.gather(
-        adjoint_rows,
-        panel_index[..., None],
-        lax.GatherDimensionNumbers(offset_dims=(2, 3), collapsed_slice_dims=(0,), start_index_map=(0,)),
-        (1, lines, cells),
-        mode=lax.GatherScatterMode.PROMISE_IN_BOUNDS,
-    )
-    picked = picked.reshape(-1, lines, cells).astype(jnp.float32)
-    edge_rows = jnp.concatenate([picked[:, :halo], picked[:, lines - halo :]], axis=0)
-    flat_index = panel_index.reshape(-1, 1)
-    picks = flat_index.shape[0]
-    own_class = jnp.broadcast_to(coef_class.astype(jnp.float32).reshape(1, 1, 1), (1, halo, cells))
-
-    def edge(rows, coef):
-        return jnp.concatenate([rows, coef[None], own_class], axis=0)
-
+    picked, down_edge, up_edge = gather_rows(adjoint_rows, panel_index, coef_class, cell_coef, halo)
     count = lax.axis_size("tile")
-    from_below = lax.ppermute(
-        edge(edge_rows[picks:], cell_coef[lines - halo :]), "tile", [(i, i + 1) for i in range(count - 1)]
-    )
-    from_above = lax.ppermute(edge(edge_rows[:picks], cell_coef[:halo]), "tile", [(i + 1, i) for i in range(count - 1)])
+    from_below = lax.ppermute(up_edge, "tile", [(i, i + 1) for i in range(count - 1)])
+    from_above = lax.ppermute(down_edge, "tile", [(i + 1, i) for i in range(count - 1)])
     classes = lax.broadcasted_iota(jnp.int32, (class_gain.shape[0], 1, 1), 0).astype(jnp.float32)
 
     def diffusion(raw_coef, class_code):

time: 42.2 us -> 41.5 us (0.983)
  local copies, waits for them, and re-layouts: 3.88 us -> 0.14 us
  Pallas kernels: 0 us -> 2.66 us
  waiting for transfers between devices: 3.31 us -> 4.87 us
  other arithmetic: 4.51 us -> 3.33 us
    pallas_call x0 -> x1, Pallas kernels: none -> 2.66 us  [gather_rows(): pl.pallas_call(functools.partial(gather_kernel, halo), out_shape=(jax.Sha...]
    gather x1 -> x0, local copies, waits for them, and re-layouts: 2.18 us -> none  [per_device(): lax.gather(adjoint_rows, panel_index[..., None], lax.GatherDimensionNumbe...]
    ppermute x2, waiting for transfers between devices: 3.31 us -> 4.87 us  [the longest x1 4.17 us: per_device(): lax.ppermute(down_edge, 'tile', [(i + 1, i) for i in range(count - 1)])]
    broadcast_in_dim x2 -> x0, local copies, waits for them, and re-layouts: 1.47 us -> none  [the longest x1 0.76 us: per_device(): panel_index[..., None]]
    reduce_sum x2, other arithmetic: 1.48 us -> 0.17 us  [diffusion(): jnp.sum(jnp.where(classes == class_code[None], class_gain[:, None, None],...]
    concatenate x1, other arithmetic: 0.06 us -> 1.01 us  [per_device(): state = jnp.concatenate([from_below[:-2], picked, from_above[:-2]], axis=1)]
    mul x2, other arithmetic: 0.71 us -> 0.01 us  [diffusion(): return 0.2 * gain * raw_coef]
  transfers between devices with their start and end apart: 2 -> 2, of which waited for: 1 -> 2; matrix products, arithmetic and copies ran while one was open for 4% -> 0% of each run, Pallas kernels for 0% -> 0%
where the time goes in v4:
time: 41.5 us; the launch traced here: 41.1 us
  blocking collectives  22.3 us (54%)
  starting transfers between devices  6.14 us (15%)
  waiting for transfers between devices  4.87 us (12%)
  other arithmetic  3.33 us (8%)
  Pallas kernels  2.66 us (6%)
  between operations  0.86 us (2%)
  matrix products  0.83 us (2%)
    all_to_all x1, blocking collectives, per_device(): parts = lax.all_to_all(terms, 'tile', 0, 0, tiled=True)  15 us
    all_gather x1, blocking collectives, per_device(): rows_piece = lax.all_gather(smoothed, 'rows', axis=1, tiled=True)  7.33 us
    ppermute x1, starting transfers between devices, per_device(): lax.ppermute(up_edge, 'tile', [(i, i + 1) for i in range(count - 1)])  4.85 us
    ppermute x1, waiting for transfers between devices, per_device(): lax.ppermute(down_edge, 'tile', [(i + 1, i) for i in range(count - 1)])  4.17 us
    pallas_call x1, Pallas kernels, gather_rows(): pl.pallas_call(functools.partial(gather_kernel, halo), out_shape=(jax.Sha...  2.66 us
    ppermute x1, starting transfers between devices, per_device(): lax.ppermute(down_edge, 'tile', [(i + 1, i) for i in range(count - 1)])  1.29 us
    concatenate x1, other arithmetic, per_device(): state = jnp.concatenate([from_below[:-2], picked, from_above[:-2]], axis=1)  1.01 us
    select_n x3, other arithmetic, per_device(): state = jnp.where(inside[None], step_core(padded, coef_pad), 0.0)  0.91 us
  transfers between devices with their start and end apart: 2, of which 2 were waited for; matrix products, arithmetic and copies ran while one was open for 0% of the time, Pallas kernels for 0%

profile of v4, /device:TPU:0, one launch (start us, length us, event | category | flops | bytes accessed | tf_op | source)
XLA Modules:
  0.0 41.1 jit_solution(8168852522782069165)
XLA Ops:
  0.0 0.0 copy-start.1
  0.0 0.0 copy-start.2
  0.7 2.7 %shard_map.55 = (f32[32,16,128]{2,1,0:T(8,128)}, f32[34,4,128]{2,1,0:T(4,128)}, f32[34,4,128]{2,1,0:T(4,128)}) custom-call(s32[2,16]{1,0:T(2,128)} %index_ref.1, s32[1]{0:T(128)S(6)} %copy.22.class_ref, bf16[512,16,128]{2,1,0:T(8,128)(2,1)} %rows_hbm.1, f32[16,128]{1,0:T(8,128)} %coef_ref.1), custom_call_target="tpu_custom_call" | custom-call | bytes 393216 | tf_op jit(solution)/shard_map/pallas_call | solution.py:42
  3.4 4.8 %collective-permute-start = (f32[34,4,128]{2,1,0:T(4,128)}, f32[34,4,128]{2,1,0:T(4,128)S(1)}, u32[]{:S(2)}, u32[]{:S(2)}) collective-permute-start(f32[34,4,128]{2,1,0:T(4,128)} %get-tuple-element.8), channel_id=1, source_target_pairs={{0,4},{4,8},{8,12},{12,16},{16,20},{20,24},{24,28},{1,5},{5,9},{9,... | collective-permute-start | bytes 208904 | tf_op jit(solution)/shard_map/ppermute | solution.py:78
  8.2 1.3 %collective-permute-start.1 = (f32[34,4,128]{2,1,0:T(4,128)}, f32[34,4,128]{2,1,0:T(4,128)S(1)}, u32[]{:S(2)}, u32[]{:S(2)}) collective-permute-start(f32[34,4,128]{2,1,0:T(4,128)} %get-tuple-element.10), channel_id=1, source_target_pairs={{4,0},{8,4},{12,8},{16,12},{20,16},{24,20},{28,24},{5,1},{9,5},{13... | collective-permute-start | bytes 208904 | tf_op jit(solution)/shard_map/ppermute | solution.py:79
  9.5 0.1 slice.143
  9.6 0.0 copy-done.2
  9.6 0.1 select_reduce_fusion
  9.7 0.0 copy-done.1
  9.7 0.7 %collective-permute-done = f32[34,4,128]{2,1,0:T(4,128)S(1)} collective-permute-done((f32[34,4,128]{2,1,0:T(4,128)}, f32[34,4,128]{2,1,0:T(4,128)S(1)}, u32[]{:S(2)}, u32[]{:S(2)}) %collective-permute-start) | collective-permute-done | bytes 69664 | tf_op jit(solution)/shard_map/ppermute | solution.py:78
  10.4 4.2 %collective-permute-done.1 = f32[34,4,128]{2,1,0:T(4,128)S(1)} collective-permute-done((f32[34,4,128]{2,1,0:T(4,128)}, f32[34,4,128]{2,1,0:T(4,128)S(1)}, u32[]{:S(2)}, u32[]{:S(2)}) %collective-permute-start.1) | collective-permute-done | bytes 69664 | tf_op jit(solution)/shard_map/ppermute | solution.py:79
  14.6 0.1 select_reduce_fusion.2
  14.7 0.1 fusion.58
  14.9 1.0 %pad_maximum_fusion = f32[32,24,128]{2,1,0:T(8,128)S(1)} fusion(f32[32,4,128]{2,1,0:T(4,128)S(1)} %slice.130, f32[32,16,128]{2,1,0:T(8,128)} %get-tuple-element.9, f32[32,4,128]{2,1,0:T(4,128)S(1)} %slice.129), kind=kLoop, calls=%fused_computation.64 | loop fusion | flops 196608 | bytes 786432 | tf_op jit(solution)/shard_map/concatenate | solution.py:87
  15.9 0.3 fusion.14
  16.2 0.3 fusion.23
  16.5 0.3 fusion.32
  16.8 0.0 copy-start
  16.8 0.3 fusion.36
  17.1 0.2 fusion.53
  17.3 7.3 %all_gather.3 = bf16[2,64,16,128]{3,2,1,0:T(8,128)(2,1)S(1)} all-gather(bf16[2,16,16,128]{3,2,1,0:T(8,128)(2,1)S(1)} %bitcast.32), channel_id=1, replica_groups=mesh['tile'=8,'rows'=4] {'rows'}, dimensions={1}, use_global_device_ids=true | all-gather | bytes 655360 | tf_op jit(solution)/shard_map/all_gather | solution.py:103
  24.7 0.0 copy-done
  24.7 0.8 %fusion.3 = f32[128,512]{1,0:T(8,128)S(1)} fusion(bf16[64,8,16,128]{3,2,1,0:T(8,128)(2,1)S(1)} %bitcast.29, bf16[16,8,16,128]{3,2,1,0:T(8,128)(2,1)S(1)} %bitcast.31), kind=kOutput, calls=%fused_computation.3 | convolution fusion | flops 268500992 | bytes 2883584 | tf_op jit(solution)/shard_map/dot_general | solution.py:106
  25.5 15.0 %all_to_all.5 = f32[8,2,8,512]{3,2,1,0:T(8,128)S(1)} all-to-all(f32[8,2,8,512]{3,2,1,0:T(8,128)S(1)} %bitcast.30), channel_id=1, replica_groups=mesh['tile'=8,'rows'=4] {'tile'}, dimensions={0} | all-to-all | bytes 524288 | tf_op jit(solution)/shard_map/all_to_all | solution.py:111
  40.5 0.6 %reduce_sum.39 = f32[2,8,512]{2,1,0:T(8,128)} reduce(f32[8,2,8,512]{3,2,1,0:T(8,128)S(1)} %all_to_all.5, f32[]{:T(128)} %constant.8.clone.1), dimensions={0}, to_apply=%region_3.4 | reduce | flops 57344 | bytes 294916 | tf_op jit(solution)/shard_map/reduce_sum | solution.py:112
  (14 shorter events, 0.1 us)
Async XLA Ops:
  0.0 9.7 %copy-start.1 = (f32[16,128]{1,0:T(8,128)S(1)}, f32[16,128]{1,0:T(8,128)}, u32[]{:S(2)}) copy-start(f32[16,128]{1,0:T(8,128)} %coef_ref.1) | copy-start | bytes 24580
  0.0 9.6 %copy-start.2 = (f32[8]{0:T(128)S(1)}, f32[8]{0:T(128)}, u32[]{:S(2)}) copy-start(f32[8]{0:T(128)} %param.8) | copy-start | bytes 100
  3.4 7.1 %collective-permute-start = (f32[34,4,128]{2,1,0:T(4,128)}, f32[34,4,128]{2,1,0:T(4,128)S(1)}, u32[]{:S(2)}, u32[]{:S(2)}) collective-permute-start(f32[34,4,128]{2,1,0:T(4,128)} %get-tuple-element.8), channel_id=1, source_target_pairs={{0,4},{4,8},{8,12},{12,16},{16,20},{20,24},{24,28},{1,5},{5,9},{9,... | collective-permute-start | bytes 208904 | tf_op jit(solution)/shard_map/ppermute | solution.py:78
  8.2 6.4 %collective-permute-start.1 = (f32[34,4,128]{2,1,0:T(4,128)}, f32[34,4,128]{2,1,0:T(4,128)S(1)}, u32[]{:S(2)}, u32[]{:S(2)}) collective-permute-start(f32[34,4,128]{2,1,0:T(4,128)} %get-tuple-element.10), channel_id=1, source_target_pairs={{4,0},{8,4},{12,8},{16,12},{20,16},{24,20},{28,24},{5,1},{9,5},{13... | collective-permute-start | bytes 208904 | tf_op jit(solution)/shard_map/ppermute | solution.py:79
  16.8 7.8 %copy-start = (bf16[512,16,128]{2,1,0:T(8,128)(2,1)S(1)}, bf16[512,16,128]{2,1,0:T(8,128)(2,1)}, u32[]{:S(2)}) copy-start(bf16[512,16,128]{2,1,0:T(8,128)(2,1)} %rows_hbm.1) | copy-start | bytes 6291460

commit v5 on v4

--- a/solution.py
+++ b/solution.py
@@ -22,8 +22,8 @@
         copies.append(copy)
     for copy in copies:
         copy.wait()
+    picked_ref[...] = buf[...]
     rows = buf[...].astype(jnp.float32)
-    picked_ref[...] = rows
     code = jnp.full(down_ref.shape[1:], class_ref[0].astype(jnp.float32), jnp.float32)
     down_ref[:count] = rows[:, :halo]
     down_ref[count] = coef_ref[:halo]
@@ -41,7 +41,7 @@
     vmem = pl.BlockSpec(memory_space=pltpu.VMEM)
     return pl.pallas_call(
         functools.partial(gather_kernel, halo),
-        out_shape=(jax.ShapeDtypeStruct((count, lines, cells), jnp.float32), edge, edge),
+        out_shape=(jax.ShapeDtypeStruct((count, lines, cells), adjoint_rows.dtype), edge, edge),
         in_specs=[smem, smem, pl.BlockSpec(memory_space=pl.ANY), vmem],
         out_specs=(vmem, vmem, vmem),
         scratch_shapes=[pltpu.VMEM((count, lines, cells), adjoint_rows.dtype), pltpu.SemaphoreType.DMA((count,))],
@@ -84,7 +84,7 @@
         return 0.2 * gain * raw_coef
 
     diffusivity = diffusion(cell_coef, jnp.broadcast_to(coef_class.astype(jnp.float32)[:, None], cell_coef.shape))
-    state = jnp.concatenate([from_below[:-2], picked, from_above[:-2]], axis=1)
+    state = jnp.concatenate([from_below[:-2], picked.astype(jnp.float32), from_above[:-2]], axis=1)
     coef_wide = jnp.concatenate(
         [diffusion(from_below[-2], from_below[-1]), diffusivity, diffusion(from_above[-2], from_above[-1])], axis=0
     )

time: 41.5 us -> 40.5 us (0.976)
  waiting for transfers between devices: 4.87 us -> 3.93 us
    concatenate x1, other arithmetic: 1.01 us -> 0.06 us  [per_device(): jnp.concatenate([from_below[:-2], picked.astype(jnp.float32), from_above[...]
    convert_element_type x0 -> x1, other arithmetic: none -> 0.92 us  [per_device(): picked.astype(jnp.float32)]
    ppermute x1, waiting for transfers between devices: 0.7 us -> 0.01 us  [per_device(): lax.ppermute(up_edge, 'tile', [(i, i + 1) for i in range(count - 1)])]
  transfers between devices with their start and end apart: 2 -> 2, of which waited for: 2 -> 1; matrix products, arithmetic and copies ran while one was open for 0% -> 3% of each run, Pallas kernels for 0% -> 0%
where the time goes in v5:
time: 40.5 us; the launch traced here: 40.2 us
  blocking collectives  22.3 us (55%)
  starting transfers between devices  6.14 us (15%)
  waiting for transfers between devices  3.93 us (10%)
  other arithmetic  3.31 us (8%)
  Pallas kernels  2.63 us (6%)
  between operations  0.87 us (2%)
  matrix products  0.83 us (2%)
    all_to_all x1, blocking collectives, per_device(): parts = lax.all_to_all(terms, 'tile', 0, 0, tiled=True)  15 us
    all_gather x1, blocking collectives, per_device(): rows_piece = lax.all_gather(smoothed, 'rows', axis=1, tiled=True)  7.33 us
    ppermute x1, starting transfers between devices, per_device(): lax.ppermute(up_edge, 'tile', [(i, i + 1) for i in range(count - 1)])  4.85 us
    ppermute x1, waiting for transfers between devices, per_device(): lax.ppermute(down_edge, 'tile', [(i + 1, i) for i in range(count - 1)])  3.93 us
    pallas_call x1, Pallas kernels, gather_rows(): pl.pallas_call(functools.partial(gather_kernel, halo), out_shape=(jax.Sha...  2.63 us
    ppermute x1, starting transfers between devices, per_device(): lax.ppermute(down_edge, 'tile', [(i + 1, i) for i in range(count - 1)])  1.29 us
    convert_element_type x1, other arithmetic, per_device(): picked.astype(jnp.float32)  0.92 us
    select_n x3, other arithmetic, per_device(): state = jnp.where(inside[None], step_core(padded, coef_pad), 0.0)  0.91 us
  transfers between devices with their start and end apart: 2, of which 1 were waited for; matrix products, arithmetic and copies ran while one was open for 3% of the time, Pallas kernels for 0%

profile of v5, /device:TPU:0, one launch (start us, length us, event | category | flops | bytes accessed | tf_op | source)
XLA Modules:
  0.0 40.2 jit_solution(11283902386375853818)
XLA Ops:
  0.0 0.0 copy-start.1
  0.0 0.0 copy-start.2
  0.7 2.6 %shard_map.55 = (bf16[32,16,128]{2,1,0:T(8,128)(2,1)}, f32[34,4,128]{2,1,0:T(4,128)}, f32[34,4,128]{2,1,0:T(4,128)}) custom-call(s32[2,16]{1,0:T(2,128)} %index_ref.1, s32[1]{0:T(128)S(6)} %copy.22.class_ref, bf16[512,16,128]{2,1,0:T(8,128)(2,1)} %rows_hbm.1, f32[16,128]{1,0:T(8,128)} %coef_ref.1), custom_call_target="tpu_custom_call" | custom-call | bytes 393216 | tf_op jit(solution)/shard_map/pallas_call | solution.py:42
  3.3 4.8 %collective-permute-start = (f32[34,4,128]{2,1,0:T(4,128)}, f32[34,4,128]{2,1,0:T(4,128)S(1)}, u32[]{:S(2)}, u32[]{:S(2)}) collective-permute-start(f32[34,4,128]{2,1,0:T(4,128)} %get-tuple-element.8), channel_id=1, source_target_pairs={{0,4},{4,8},{8,12},{12,16},{16,20},{20,24},{24,28},{1,5},{5,9},{9,... | collective-permute-start | bytes 208904 | tf_op jit(solution)/shard_map/ppermute | solution.py:78
  8.2 1.3 %collective-permute-start.1 = (f32[34,4,128]{2,1,0:T(4,128)}, f32[34,4,128]{2,1,0:T(4,128)S(1)}, u32[]{:S(2)}, u32[]{:S(2)}) collective-permute-start(f32[34,4,128]{2,1,0:T(4,128)} %get-tuple-element.10), channel_id=1, source_target_pairs={{4,0},{8,4},{12,8},{16,12},{20,16},{24,20},{28,24},{5,1},{9,5},{13... | collective-permute-start | bytes 208904 | tf_op jit(solution)/shard_map/ppermute | solution.py:79
  9.5 0.1 slice.143
  9.6 0.0 copy-done.2
  9.6 0.1 select_reduce_fusion
  9.7 0.0 copy-done.1
  9.7 0.9 %convert_element_type.36 = f32[32,16,128]{2,1,0:T(8,128)S(1)} convert(bf16[32,16,128]{2,1,0:T(8,128)(2,1)} %get-tuple-element.9) | non-fusion elementwise | flops 65536 | bytes 393216 | tf_op jit(solution)/shard_map/convert_element_type | solution.py:87
  10.6 0.0 collective-permute-done
  10.7 3.9 %collective-permute-done.1 = f32[34,4,128]{2,1,0:T(4,128)S(1)} collective-permute-done((f32[34,4,128]{2,1,0:T(4,128)}, f32[34,4,128]{2,1,0:T(4,128)S(1)}, u32[]{:S(2)}, u32[]{:S(2)}) %collective-permute-start.1) | collective-permute-done | bytes 69664 | tf_op jit(solution)/shard_map/ppermute | solution.py:79
  14.6 0.1 select_reduce_fusion.2
  14.7 0.1 fusion.58
  14.8 0.1 pad_maximum_fusion
  14.9 0.3 fusion.14
  15.2 0.3 fusion.23
  15.5 0.3 fusion.32
  15.8 0.0 copy-start
  15.9 0.3 fusion.36
  16.1 0.2 fusion.53
  16.3 7.3 %all_gather.3 = bf16[2,64,16,128]{3,2,1,0:T(8,128)(2,1)S(1)} all-gather(bf16[2,16,16,128]{3,2,1,0:T(8,128)(2,1)S(1)} %bitcast.32), channel_id=1, replica_groups=mesh['tile'=8,'rows'=4] {'rows'}, dimensions={1}, use_global_device_ids=true | all-gather | bytes 655360 | tf_op jit(solution)/shard_map/all_gather | solution.py:103
  23.7 0.0 copy-done
  23.7 0.8 %fusion.3 = f32[128,512]{1,0:T(8,128)S(1)} fusion(bf16[64,8,16,128]{3,2,1,0:T(8,128)(2,1)S(1)} %bitcast.29, bf16[16,8,16,128]{3,2,1,0:T(8,128)(2,1)S(1)} %bitcast.31), kind=kOutput, calls=%fused_computation.3 | convolution fusion | flops 268500992 | bytes 2883584 | tf_op jit(solution)/shard_map/dot_general | solution.py:106
  24.5 15.0 %all_to_all.5 = f32[8,2,8,512]{3,2,1,0:T(8,128)S(1)} all-to-all(f32[8,2,8,512]{3,2,1,0:T(8,128)S(1)} %bitcast.30), channel_id=1, replica_groups=mesh['tile'=8,'rows'=4] {'tile'}, dimensions={0} | all-to-all | bytes 524288 | tf_op jit(solution)/shard_map/all_to_all | solution.py:111
  39.5 0.6 %reduce_sum.39 = f32[2,8,512]{2,1,0:T(8,128)} reduce(f32[8,2,8,512]{3,2,1,0:T(8,128)S(1)} %all_to_all.5, f32[]{:T(128)} %constant.8.clone.1), dimensions={0}, to_apply=%region_3.4 | reduce | flops 57344 | bytes 294916 | tf_op jit(solution)/shard_map/reduce_sum | solution.py:112
  (14 shorter events, 0.1 us)
Async XLA Ops:
  0.0 9.7 %copy-start.1 = (f32[16,128]{1,0:T(8,128)S(1)}, f32[16,128]{1,0:T(8,128)}, u32[]{:S(2)}) copy-start(f32[16,128]{1,0:T(8,128)} %coef_ref.1) | copy-start | bytes 24580
  0.0 9.6 %copy-start.2 = (f32[8]{0:T(128)S(1)}, f32[8]{0:T(128)}, u32[]{:S(2)}) copy-start(f32[8]{0:T(128)} %param.8) | copy-start | bytes 100
  3.3 7.3 %collective-permute-start = (f32[34,4,128]{2,1,0:T(4,128)}, f32[34,4,128]{2,1,0:T(4,128)S(1)}, u32[]{:S(2)}, u32[]{:S(2)}) collective-permute-start(f32[34,4,128]{2,1,0:T(4,128)} %get-tuple-element.8), channel_id=1, source_target_pairs={{0,4},{4,8},{8,12},{12,16},{16,20},{20,24},{24,28},{1,5},{5,9},{9,... | collective-permute-start | bytes 208904 | tf_op jit(solution)/shard_map/ppermute | solution.py:78
  8.2 6.4 %collective-permute-start.1 = (f32[34,4,128]{2,1,0:T(4,128)}, f32[34,4,128]{2,1,0:T(4,128)S(1)}, u32[]{:S(2)}, u32[]{:S(2)}) collective-permute-start(f32[34,4,128]{2,1,0:T(4,128)} %get-tuple-element.10), channel_id=1, source_target_pairs={{4,0},{8,4},{12,8},{16,12},{20,16},{24,20},{28,24},{5,1},{9,5},{13... | collective-permute-start | bytes 208904 | tf_op jit(solution)/shard_map/ppermute | solution.py:79
  15.8 7.8 %copy-start = (bf16[512,16,128]{2,1,0:T(8,128)(2,1)S(1)}, bf16[512,16,128]{2,1,0:T(8,128)(2,1)}, u32[]{:S(2)}) copy-start(bf16[512,16,128]{2,1,0:T(8,128)(2,1)} %rows_hbm.1) | copy-start | bytes 6291460

commit v6 on v5

--- a/solution.py
+++ b/solution.py
@@ -11,17 +11,12 @@
 SMOOTH = 4
 
 
-def gather_kernel(halo, index_ref, class_ref, rows_hbm, coef_ref, picked_ref, down_ref, up_ref, buf, sems):
+def gather_kernel(halo, index_ref, class_ref, rows_ref, coef_ref, picked_ref, down_ref, up_ref, buf):
     panels, per_block = index_ref.shape
     count = panels * per_block
     lines = buf.shape[1]
-    copies = []
     for i in range(count):
-        copy = pltpu.make_async_copy(rows_hbm.at[index_ref[i // per_block, i % per_block]], buf.at[i], sems.at[i])
-        copy.start()
-        copies.append(copy)
-    for copy in copies:
-        copy.wait()
+        buf[i] = rows_ref[index_ref[i // per_block, i % per_block]]
     picked_ref[...] = buf[...]
     rows = buf[...].astype(jnp.float32)
     code = jnp.full(down_ref.shape[1:], class_ref[0].astype(jnp.float32), jnp.float32)
@@ -42,9 +37,9 @@
     return pl.pallas_call(
         functools.partial(gather_kernel, halo),
         out_shape=(jax.ShapeDtypeStruct((count, lines, cells), adjoint_rows.dtype), edge, edge),
-        in_specs=[smem, smem, pl.BlockSpec(memory_space=pl.ANY), vmem],
+        in_specs=[smem, smem, vmem, vmem],
         out_specs=(vmem, vmem, vmem),
-        scratch_shapes=[pltpu.VMEM((count, lines, cells), adjoint_rows.dtype), pltpu.SemaphoreType.DMA((count,))],
+        scratch_shapes=[pltpu.VMEM((count, lines, cells), adjoint_rows.dtype)],
         cost_estimate=pl.CostEstimate(flops=0, transcendentals=0, bytes_accessed=count * lines * cells * 6),
     )(panel_index, coef_class, adjoint_rows, cell_coef)
 

time: 40.5 us -> 40.1 us (level)
  no operation moved by 1% of the time
where the time goes in v6:
time: 40.1 us; the launch traced here: 39.9 us
  blocking collectives  22.3 us (56%)
  starting transfers between devices  6.13 us (15%)
  waiting for transfers between devices  3.93 us (10%)
  other arithmetic  3.31 us (8%)
  Pallas kernels  2.35 us (6%)
  between operations  0.86 us (2%)
  matrix products  0.83 us (2%)
    all_to_all x1, blocking collectives, per_device(): parts = lax.all_to_all(terms, 'tile', 0, 0, tiled=True)  15 us
    all_gather x1, blocking collectives, per_device(): rows_piece = lax.all_gather(smoothed, 'rows', axis=1, tiled=True)  7.33 us
    ppermute x1, starting transfers between devices, per_device(): lax.ppermute(up_edge, 'tile', [(i, i + 1) for i in range(count - 1)])  4.83 us
    ppermute x1, waiting for transfers between devices, per_device(): lax.ppermute(down_edge, 'tile', [(i + 1, i) for i in range(count - 1)])  3.93 us
    pallas_call x1, Pallas kernels, gather_rows(): pl.pallas_call(functools.partial(gather_kernel, halo), out_shape=(jax.Sha...  2.35 us
    ppermute x1, starting transfers between devices, per_device(): lax.ppermute(down_edge, 'tile', [(i + 1, i) for i in range(count - 1)])  1.29 us
    convert_element_type x1, other arithmetic, per_device(): picked.astype(jnp.float32)  0.92 us
    select_n x3, other arithmetic, per_device(): state = jnp.where(inside[None], step_core(padded, coef_pad), 0.0)  0.91 us
  transfers between devices with their start and end apart: 2, of which 1 were waited for; matrix products, arithmetic and copies ran while one was open for 3% of the time, Pallas kernels for 0%

profile of v6, /device:TPU:0, one launch (start us, length us, event | category | flops | bytes accessed | tf_op | source)
XLA Modules:
  0.0 39.9 jit_solution(5793123579959270577)
XLA Ops:
  0.0 0.0 copy-start.1
  0.0 0.0 copy-start.2
  0.7 2.4 %shard_map.55 = (bf16[32,16,128]{2,1,0:T(8,128)(2,1)}, f32[34,4,128]{2,1,0:T(4,128)}, f32[34,4,128]{2,1,0:T(4,128)}) custom-call(s32[2,16]{1,0:T(2,128)} %index_ref.1, s32[1]{0:T(128)S(6)} %copy.22.class_ref, bf16[512,16,128]{2,1,0:T(8,128)(2,1)} %rows_ref.1, f32[16,128]{1,0:T(8,128)} %coef_ref.1), custom_call_target="tpu_custom_call" | custom-call | bytes 393216 | tf_op jit(solution)/shard_map/pallas_call | solution.py:37
  3.0 4.8 %collective-permute-start = (f32[34,4,128]{2,1,0:T(4,128)}, f32[34,4,128]{2,1,0:T(4,128)S(1)}, u32[]{:S(2)}, u32[]{:S(2)}) collective-permute-start(f32[34,4,128]{2,1,0:T(4,128)} %get-tuple-element.8), channel_id=1, source_target_pairs={{0,4},{4,8},{8,12},{12,16},{16,20},{20,24},{24,28},{1,5},{5,9},{9,... | collective-permute-start | bytes 208904 | tf_op jit(solution)/shard_map/ppermute | solution.py:73
  7.9 1.3 %collective-permute-start.1 = (f32[34,4,128]{2,1,0:T(4,128)}, f32[34,4,128]{2,1,0:T(4,128)S(1)}, u32[]{:S(2)}, u32[]{:S(2)}) collective-permute-start(f32[34,4,128]{2,1,0:T(4,128)} %get-tuple-element.10), channel_id=1, source_target_pairs={{4,0},{8,4},{12,8},{16,12},{20,16},{24,20},{28,24},{5,1},{9,5},{13... | collective-permute-start | bytes 208904 | tf_op jit(solution)/shard_map/ppermute | solution.py:74
  9.2 0.1 slice.143
  9.3 0.0 copy-done.2
  9.3 0.1 select_reduce_fusion
  9.4 0.0 copy-done.1
  9.4 0.9 %convert_element_type.36 = f32[32,16,128]{2,1,0:T(8,128)S(1)} convert(bf16[32,16,128]{2,1,0:T(8,128)(2,1)} %get-tuple-element.9) | non-fusion elementwise | flops 65536 | bytes 393216 | tf_op jit(solution)/shard_map/convert_element_type | solution.py:82
  10.3 0.0 collective-permute-done
  10.4 3.9 %collective-permute-done.1 = f32[34,4,128]{2,1,0:T(4,128)S(1)} collective-permute-done((f32[34,4,128]{2,1,0:T(4,128)}, f32[34,4,128]{2,1,0:T(4,128)S(1)}, u32[]{:S(2)}, u32[]{:S(2)}) %collective-permute-start.1) | collective-permute-done | bytes 69664 | tf_op jit(solution)/shard_map/ppermute | solution.py:74
  14.3 0.1 select_reduce_fusion.2
  14.4 0.1 fusion.58
  14.5 0.1 pad_maximum_fusion
  14.6 0.3 fusion.14
  14.9 0.3 fusion.23
  15.2 0.3 fusion.32
  15.5 0.0 copy-start
  15.6 0.3 fusion.36
  15.9 0.2 fusion.53
  16.0 7.3 %all_gather.3 = bf16[2,64,16,128]{3,2,1,0:T(8,128)(2,1)S(1)} all-gather(bf16[2,16,16,128]{3,2,1,0:T(8,128)(2,1)S(1)} %bitcast.32), channel_id=1, replica_groups=mesh['tile'=8,'rows'=4] {'rows'}, dimensions={1}, use_global_device_ids=true | all-gather | bytes 655360 | tf_op jit(solution)/shard_map/all_gather | solution.py:98
  23.4 0.0 copy-done
  23.4 0.8 %fusion.3 = f32[128,512]{1,0:T(8,128)S(1)} fusion(bf16[64,8,16,128]{3,2,1,0:T(8,128)(2,1)S(1)} %bitcast.29, bf16[16,8,16,128]{3,2,1,0:T(8,128)(2,1)S(1)} %bitcast.31), kind=kOutput, calls=%fused_computation.3 | convolution fusion | flops 268500992 | bytes 2883584 | tf_op jit(solution)/shard_map/dot_general | solution.py:101
  24.2 15.0 %all_to_all.5 = f32[8,2,8,512]{3,2,1,0:T(8,128)S(1)} all-to-all(f32[8,2,8,512]{3,2,1,0:T(8,128)S(1)} %bitcast.30), channel_id=1, replica_groups=mesh['tile'=8,'rows'=4] {'tile'}, dimensions={0} | all-to-all | bytes 524288 | tf_op jit(solution)/shard_map/all_to_all | solution.py:106
  39.2 0.6 %reduce_sum.39 = f32[2,8,512]{2,1,0:T(8,128)} reduce(f32[8,2,8,512]{3,2,1,0:T(8,128)S(1)} %all_to_all.5, f32[]{:T(128)} %constant.8.clone.1), dimensions={0}, to_apply=%region_3.4 | reduce | flops 57344 | bytes 294916 | tf_op jit(solution)/shard_map/reduce_sum | solution.py:107
  (14 shorter events, 0.1 us)
Async XLA Ops:
  0.0 9.4 %copy-start.1 = (f32[16,128]{1,0:T(8,128)S(1)}, f32[16,128]{1,0:T(8,128)}, u32[]{:S(2)}) copy-start(f32[16,128]{1,0:T(8,128)} %coef_ref.1) | copy-start | bytes 24580
  0.0 9.3 %copy-start.2 = (f32[8]{0:T(128)S(1)}, f32[8]{0:T(128)}, u32[]{:S(2)}) copy-start(f32[8]{0:T(128)} %param.8) | copy-start | bytes 100
  3.0 7.3 %collective-permute-start = (f32[34,4,128]{2,1,0:T(4,128)}, f32[34,4,128]{2,1,0:T(4,128)S(1)}, u32[]{:S(2)}, u32[]{:S(2)}) collective-permute-start(f32[34,4,128]{2,1,0:T(4,128)} %get-tuple-element.8), channel_id=1, source_target_pairs={{0,4},{4,8},{8,12},{12,16},{16,20},{20,24},{24,28},{1,5},{5,9},{9,... | collective-permute-start | bytes 208904 | tf_op jit(solution)/shard_map/ppermute | solution.py:73
  7.9 6.4 %collective-permute-start.1 = (f32[34,4,128]{2,1,0:T(4,128)}, f32[34,4,128]{2,1,0:T(4,128)S(1)}, u32[]{:S(2)}, u32[]{:S(2)}) collective-permute-start(f32[34,4,128]{2,1,0:T(4,128)} %get-tuple-element.10), channel_id=1, source_target_pairs={{4,0},{8,4},{12,8},{16,12},{20,16},{24,20},{28,24},{5,1},{9,5},{13... | collective-permute-start | bytes 208904 | tf_op jit(solution)/shard_map/ppermute | solution.py:74
  15.5 7.8 %copy-start = (bf16[512,16,128]{2,1,0:T(8,128)(2,1)S(1)}, bf16[512,16,128]{2,1,0:T(8,128)(2,1)}, u32[]{:S(2)}) copy-start(bf16[512,16,128]{2,1,0:T(8,128)(2,1)} %rows_ref.1) | copy-start | bytes 6291460
